TPU v7x, 256 devices: a whole 4x4x8 slice. The times are simulated.
256 devices in a mesh: seq: 64 (over z, x, core), head: 4 (over y).
Axes of the slice: x: 4, y: 4, z: 8, core: 2. Of those that a mesh axis runs over, the one named last changes fastest.
Arguments:
- queries: bfloat16 [32768, 1536], P('seq', 'head'), may hold values from -6 to 6
- keys: bfloat16 [32768, 1536], P('seq', 'head'), may hold values from -6 to 6
- values: bfloat16 [32768, 1536], P('seq', 'head'), may hold values from -6 to 6
- out_weight: bfloat16 [1536, 1536], P('head'), may hold values from -0.625 to 0.625
- cotangent: bfloat16 [32768, 1536], P('seq', 'head'), may hold values from -6 to 6
- routes: int32 [64, 2], replicated, may hold values from 0 to 63, as said below
- shot_ids: int32 [32768], P('seq'), may hold values from 0 to 31, never falling along the last dimension, each value on 1 to 2048 neighbouring positions
Outputs:
- attn_out: bfloat16 [32768, 1536], P('seq', 'head')
- grad_queries: bfloat16 [32768, 1536], P('seq', 'head')
- grad_keys: bfloat16 [32768, 1536], P('seq', 'head')
- grad_values: bfloat16 [32768, 1536], P('seq', 'head')
Inputs may be any that keep to these rules, and one draw needn't show every extreme that they name: routes[c, j] names a block of another device whose index of seq differs from that of block c by at most 2; the 2 routes of the blocks of one device name blocks of distinct devices.
All inputs are finite; a program needn't handle non-finite values.
Results may differ from a plain program's by a relative error of at most 0.025.
Values may be sent and summed in bfloat16 or wider, within the bound.
No kernel may reach another device: no remote copies, remote signals or barrier semaphores. Data moves between devices by JAX's collectives and lax.ppermute only.
A program may use at most 64 MiB of HBM per device.

v0:
```python
import jax
import jax.numpy as jnp
from jax import lax
from jax.sharding import PartitionSpec as P

HEAD_DIM = 128
BLOCK_LEN = 512


def shifted(block, axis, distance):
    devices = range(lax.axis_size(axis))
    route = [(i - distance, i) for i in devices if i - distance in devices]
    return lax.ppermute(block, axis, route)


def fold_cotangent(weight_rows, piece):
    return lax.dot_general(
        piece, weight_rows, (((1,), (1,)), ((), ())), preferred_element_type=jnp.float32
    )


def fetch_shards(pair, offset_dev):
    return shifted((pair[0], pair[1]), "seq", offset_dev)


def return_tiles(pair, offset_dev):
    return shifted((pair[0], pair[1]), "seq", offset_dev)


def add_block(running, block_slot, addend):
    current = lax.dynamic_index_in_dim(running, block_slot, 0, keepdims=False)
    return lax.dynamic_update_index_in_dim(
        running, current + addend.astype(jnp.float32), block_slot, 0
    )


def on_device(queries, keys, values, out_weight, cotangent, routes, shot_ids):
    seq_count = lax.axis_size("seq")
    seq_index = lax.axis_index("seq")
    tok_rows, columns = queries.shape
    block_len = BLOCK_LEN
    per_device = tok_rows // block_len
    reach_devs = max(2, 2 * per_device)
    heads_here = columns // HEAD_DIM
    score_scale = HEAD_DIM ** (-0.5)
    offsets_all = [
        offset_dev for offset_dev in range(-reach_devs, reach_devs + 1) if offset_dev != 0
    ]
    grad_attn = fold_cotangent(
        out_weight, lax.all_gather(cotangent, "head", axis=1, tiled=True)
    ).astype(jnp.bfloat16)
    own_routes = lax.dynamic_slice_in_dim(routes, seq_index * per_device, per_device, 0)
    route_owner = own_routes // per_device - seq_index
    route_slot = jnp.where(route_owner < 0, route_owner + reach_devs, route_owner + reach_devs - 1)
    route_block = own_routes % per_device
    served = []
    for offset_dev in offsets_all:
        reader = jnp.clip(seq_index - offset_dev, 0, seq_count - 1)
        asked = lax.dynamic_slice_in_dim(routes, reader * per_device, per_device, 0)
        owned = asked // per_device == seq_index
        served.append(jnp.sum(jnp.where(owned, asked % per_device, 0)))
    recv_keys = []
    recv_values = []
    for offset_dev in offsets_all:
        got_keys, got_values = fetch_shards((keys, values), -offset_dev)
        recv_keys.append(got_keys.reshape(per_device, block_len, columns))
        recv_values.append(got_values.reshape(per_device, block_len, columns))
    pick_index = route_slot * per_device + route_block
    routed_keys = jnp.take(jnp.concatenate(recv_keys, axis=0), pick_index, axis=0)
    routed_values = jnp.take(jnp.concatenate(recv_values, axis=0), pick_index, axis=0)
    query_blocks = queries.reshape(per_device, block_len, heads_here, HEAD_DIM)
    key_blocks = keys.reshape(per_device, block_len, heads_here, HEAD_DIM)
    value_blocks = values.reshape(per_device, block_len, heads_here, HEAD_DIM)
    grad_blocks = grad_attn.reshape(per_device, block_len, heads_here, HEAD_DIM)
    shot_blocks = shot_ids.reshape(per_device, block_len)
    self_k = key_blocks[0]
    self_v = value_blocks[0]
    route_k = routed_keys[0].reshape(2 * block_len, heads_here, HEAD_DIM)
    route_v = routed_values[0].reshape(2 * block_len, heads_here, HEAD_DIM)
    query_rows = query_blocks[0]
    grad_rows = grad_blocks[0]
    shots_here = shot_blocks[0]
    same_shot = shots_here[:, None] == shots_here[None, :]
    scores_self = (
        jnp.einsum("qhd,khd->hqk", query_rows, self_k, preferred_element_type=jnp.float32)
        * score_scale
    )
    scores_self = jnp.where(same_shot[None], scores_self, -1e30)
    scores_route = (
        jnp.einsum("qhd,khd->hqk", query_rows, route_k, preferred_element_type=jnp.float32)
        * score_scale
    )
    row_top = jnp.maximum(
        jnp.max(scores_self, axis=2, keepdims=True), jnp.max(scores_route, axis=2, keepdims=True)
    )
    weights_self = jnp.exp(scores_self - row_top)
    weights_route = jnp.exp(scores_route - row_top)
    row_total = jnp.sum(weights_self, axis=2, keepdims=True) + jnp.sum(
        weights_route, axis=2, keepdims=True
    )
    probs_self = weights_self / row_total
    probs_route = weights_route / row_total
    low_self = probs_self.astype(jnp.bfloat16)
    low_route = probs_route.astype(jnp.bfloat16)
    attn_acc = jnp.einsum("hqk,khd->qhd", low_self, self_v, preferred_element_type=jnp.float32)
    attn_acc = attn_acc + jnp.einsum(
        "hqk,khd->qhd", low_route, route_v, preferred_element_type=jnp.float32
    )
    attn_rows = attn_acc.astype(jnp.bfloat16)
    row_dot = jnp.einsum(
        "qhd,qhd->hq", attn_rows.astype(jnp.float32), grad_rows.astype(jnp.float32)
    )
    dprobs_self = jnp.einsum("qhd,khd->hqk", grad_rows, self_v, preferred_element_type=jnp.float32)
    dprobs_route = jnp.einsum(
        "qhd,khd->hqk", grad_rows, route_v, preferred_element_type=jnp.float32
    )
    dscores_self = (probs_self * (dprobs_self - row_dot[:, :, None]) * score_scale).astype(
        jnp.bfloat16
    )
    dscores_route = (probs_route * (dprobs_route - row_dot[:, :, None]) * score_scale).astype(
        jnp.bfloat16
    )
    query_acc = jnp.einsum("hqk,khd->qhd", dscores_self, self_k, preferred_element_type=jnp.float32)
    query_acc = query_acc + jnp.einsum(
        "hqk,khd->qhd", dscores_route, route_k, preferred_element_type=jnp.float32
    )
    grad_query = query_acc.astype(jnp.bfloat16)
    key_self = jnp.einsum(
        "hqk,qhd->khd", dscores_self, query_rows, preferred_element_type=jnp.float32
    ).reshape(block_len, columns)
    key_route = jnp.einsum(
        "hqk,qhd->khd", dscores_route, query_rows, preferred_element_type=jnp.float32
    ).reshape(2, block_len, columns)
    value_self = jnp.einsum(
        "hqk,qhd->khd", low_self, grad_rows, preferred_element_type=jnp.float32
    ).reshape(block_len, columns)
    value_route = jnp.einsum(
        "hqk,qhd->khd", low_route, grad_rows, preferred_element_type=jnp.float32
    ).reshape(2, block_len, columns)
    attn_list = attn_rows.reshape(block_len, columns)
    query_grads = grad_query.reshape(block_len, columns)
    self_keys = [key_self]
    self_values = [value_self]
    sent_keys = key_route.astype(jnp.bfloat16)
    sent_values = value_route.astype(jnp.bfloat16)
    partial_term = jnp.dot(attn_list, out_weight, preferred_element_type=jnp.float32)
    attn_out = lax.psum_scatter(
        partial_term.astype(jnp.bfloat16), "head", scatter_dimension=1, tiled=True
    )
    key_sums = jnp.stack(self_keys)
    value_sums = jnp.stack(self_values)
    flat_owner = route_owner.reshape(-1)
    slot_ids = jnp.arange(2 * per_device, dtype=jnp.int32)
    zero_tile = jnp.zeros((block_len, columns), jnp.bfloat16)
    for position, offset_dev in enumerate(offsets_all):
        matches = flat_owner == offset_dev
        slot_index = jnp.sum(jnp.where(matches, slot_ids, 0))
        any_match = jnp.any(matches)
        part_keys = jnp.where(any_match, sent_keys[slot_index], zero_tile)
        part_values = jnp.where(any_match, sent_values[slot_index], zero_tile)
        back_keys, back_values = return_tiles((part_keys, part_values), offset_dev)
        key_sums = add_block(key_sums, served[position], back_keys)
        value_sums = add_block(value_sums, served[position], back_values)
    grad_keys = key_sums.reshape(tok_rows, columns).astype(jnp.bfloat16)
    grad_values = value_sums.reshape(tok_rows, columns).astype(jnp.bfloat16)
    return (attn_out, query_grads, grad_keys, grad_values)


def solution(mesh):
    in_specs = (
        P("seq", "head"),
        P("seq", "head"),
        P("seq", "head"),
        P("head", None),
        P("seq", "head"),
        P(),
        P("seq"),
    )
    out_specs = (P("seq", "head"), P("seq", "head"), P("seq", "head"), P("seq", "head"))
    return jax.shard_map(
        on_device, mesh=mesh, in_specs=in_specs, out_specs=out_specs, check_vma=False
    )
```

profile of v0, /device:TPU:111, one launch (start us, length us, event | category | flops | bytes accessed | tf_op | source)
XLA Modules:
  0.0 208.3 jit_solution(11243333578120095968)
XLA Ops:
  7.2 4.8 %collective-permute-start = (bf16[512,384]{1,0:T(8,128)(2,1)}, bf16[512,384]{1,0:T(8,128)(2,1)S(1)}, u32[]{:S(2)}, u32[]{:S(2)}) collective-permute-start(bf16[512,384]{1,0:T(8,128)(2,1)} %param.10), channel_id=1, source_target_pairs={{0,8},{4,12},{8,16},{12,20},{16,24},{20,28},{24,32},{28,36},{32,40... | collective-permute-start | bytes 1179656 | tf_op jit(solution)/shard_map/ppermute | solution.py:13
  12.0 4.0 %collective-permute-start.1 = (bf16[512,384]{1,0:T(8,128)(2,1)}, bf16[512,384]{1,0:T(8,128)(2,1)S(1)}, u32[]{:S(2)}, u32[]{:S(2)}) collective-permute-start(bf16[512,384]{1,0:T(8,128)(2,1)} %param.10), channel_id=1, source_target_pairs={{0,4},{4,8},{8,12},{12,16},{16,20},{20,24},{24,28},{28,32},{32,36}... | collective-permute-start | bytes 1179656 | tf_op jit(solution)/shard_map/ppermute | solution.py:13
  20.1 6.4 %collective-permute-start.4 = (bf16[512,384]{1,0:T(8,128)(2,1)}, bf16[512,384]{1,0:T(8,128)(2,1)S(1)}, u32[]{:S(2)}, u32[]{:S(2)}) collective-permute-start(bf16[512,384]{1,0:T(8,128)(2,1)} %param.11), channel_id=1, source_target_pairs={{0,8},{4,12},{8,16},{12,20},{16,24},{20,28},{24,32},{28,36},{32,40... | collective-permute-start | bytes 1179656 | tf_op jit(solution)/shard_map/ppermute | solution.py:13
  42.6 4.2 %collective-permute-start.5 = (bf16[512,384]{1,0:T(8,128)(2,1)}, bf16[512,384]{1,0:T(8,128)(2,1)}, u32[]{:S(2)}, u32[]{:S(2)}) collective-permute-start(bf16[512,384]{1,0:T(8,128)(2,1)} %param.11), channel_id=1, source_target_pairs={{0,4},{4,8},{8,12},{12,16},{16,20},{20,24},{24,28},{28,32},{32,36}... | collective-permute-start | bytes 1179656 | tf_op jit(solution)/shard_map/ppermute | solution.py:13
  50.9 2.5 %fusion.3 = (f32[3,512]{1,0:T(4,128)S(1)}, f32[3,512,512]{1,2,0:T(8,128)}) fusion(pred[512,512]{0,1:T(8,128)(4,1)S(1)} %broadcast_compare_fusion, bf16[512,3,128]{0,2,1:T(8,128)(2,1)S(1)} %bitcast.111, bf16[512,3,128]{0,2,1:T(8,128)(2,1)S(1)} %bitcast.116), kind=kOutput, calls=%fused_computation.12 | convolution fusion | flops 203684352 | bytes 4200448 | tf_op jit(solution)/shard_map/qhd,khd->hqk/dot_general | solution.py:85
  53.4 2.5 %pad_maximum_fusion = bf16[4,512,384]{2,1,0:T(8,128)(2,1)} fusion(bf16[1,512,384]{2,1,0:T(8,128)(2,1)} %bitcast.7, bf16[1,512,384]{2,1,0:T(8,128)(2,1)} %bitcast.6, bf16[1,512,384]{2,1,0:T(8,128)(2,1)S(1)} %bitcast.123, bf16[1,512,384]{2,1,0:T(8,128)(2,1)S(1)} %bitcast.122), kind=kLoop, calls=%fused_computation.15 | loop fusion | flops 2359296 | bytes 3145728 | tf_op jit(solution)/shard_map/concatenate | solution.py:69
  58.1 4.3 %collective-permute-done.6 = bf16[512,384]{1,0:T(8,128)(2,1)} collective-permute-done((bf16[512,384]{1,0:T(8,128)(2,1)}, bf16[512,384]{1,0:T(8,128)(2,1)}, u32[]{:S(2)}, u32[]{:S(2)}) %collective-permute-start.6) | collective-permute-done | bytes 393248 | tf_op jit(solution)/shard_map/ppermute | solution.py:13
  62.4 3.0 %collective-permute-done.7 = bf16[512,384]{1,0:T(8,128)(2,1)} collective-permute-done((bf16[512,384]{1,0:T(8,128)(2,1)}, bf16[512,384]{1,0:T(8,128)(2,1)}, u32[]{:S(2)}, u32[]{:S(2)}) %collective-permute-start.7) | collective-permute-done | bytes 393248 | tf_op jit(solution)/shard_map/ppermute | solution.py:13
  65.4 2.6 %pad_maximum_fusion.1 = bf16[4,512,384]{2,1,0:T(8,128)(2,1)} fusion(bf16[1,512,384]{2,1,0:T(8,128)(2,1)} %bitcast.15, bf16[1,512,384]{2,1,0:T(8,128)(2,1)} %bitcast.14, bf16[1,512,384]{2,1,0:T(8,128)(2,1)} %bitcast.13, bf16[1,512,384]{2,1,0:T(8,128)(2,1)S(1)} %bitcast.121), kind=kLoop, calls=%fused_computation.16 | loop fusion | flops 2359296 | bytes 3145728 | tf_op jit(solution)/shard_map/concatenate | solution.py:70
  74.5 2.5 %copy.367 = bf16[1,2,512,384]{2,1,3,0:T(2,128)(2,1)S(1)} copy(bf16[1,2,512,384]{3,2,1,0:T(8,128)(2,1)} %get-tuple-element.63) | data formatting | bytes 1572864 | tf_op jit(solution)/shard_map/jit(_take)/select_n | solution.py:70
  87.3 5.2 %fusion.14 = bf16[1024,3,128]{0,2,1:T(8,128)(2,1)} fusion(bf16[512,3,128]{0,2,1:T(8,128)(2,1)S(1)} %bitcast.131, f32[3,1024,512]{2,1,0:T(8,128)} %copy-done.1, f32[3,512]{1,0:T(4,128)S(1)} %add.115, f32[3,512]{1,0:T(4,128)S(1)} %max.13), kind=kOutput, calls=%fused_computation.32 | convolution fusion | flops 409337856 | bytes 7483392 | tf_op jit(solution)/shard_map/hqk,qhd->khd/dot_general | solution.py:137
  92.5 3.4 %convert_element_type.92 = bf16[2,512,384]{1,0,2:T(2,128)(2,1)} reshape(bf16[1024,3,128]{0,2,1:T(8,128)(2,1)} %fusion.14) | data formatting | bytes 1572864 | tf_op jit(solution)/shard_map/convert_element_type | solution.py:145
  95.9 4.9 %fusion.28 = (f32[3,512]{1,0:T(4,128)S(1)}, bf16[512,3,128]{0,2,1:T(8,128)(2,1)S(1)}) fusion(bf16[3,512,128]{1,2,0:T(8,128)(2,1)} %bitcast.132, f32[512,3,128]{0,2,1:T(8,128)} %convolution_bitcast_fusion.1, bf16[1024,3,128]{0,2,1:T(8,128)(2,1)} %reshape_squeeze.7, f32[3,512]{1,0:T(4,128)S(1)} %add.115, f32[3,512]{1,0:T(4,128)S(1)} %max.13, ...), kind=kOutput, calls=%fused_computation.43 | convolution fusion | flops 410122752 | bytes 8669184 | tf_op jit(solution)/shard_map/hqk,khd->qhd/dot_general | solution.py:106
  100.9 2.5 %multiply_convert_fusion = bf16[3,512,1024]{1,2,0:T(8,128)(2,1)S(1)} fusion(f32[3,512]{1,0:T(4,128)S(1)} %get-tuple-element.69, bf16[512,3,128]{0,2,1:T(8,128)(2,1)S(1)} %bitcast.134, bf16[1024,3,128]{0,2,1:T(8,128)(2,1)S(1)} %copy-done.18, f32[3,512]{1,0:T(4,128)S(1)} %add.115, f32[3,512]{1,0:T(4,128)S(1)} %max.13, f32[3,1024,512]{2,1,0:T(8,128)S(1)} %bitcast.110), kind=kOutput, calls=%fused_computation.5 | convolution fusion | flops 413663232 | bytes 10635264 | tf_op jit(solution)/shard_map/qhd,khd->hqk/dot_general | solution.py:114
  108.0 7.8 %broadcast_select_fusion.6 = (bf16[1,512,384]{1,0,2:T(2,128)(2,1)}, bf16[1,512,384]{1,0,2:T(2,128)(2,1)S(1)}, bf16[1,512,384]{1,0,2:T(2,128)(2,1)}, bf16[1,512,384]{1,0,2:T(2,128)(2,1)}) fusion(pred[]{:T(512)} %get-tuple-element.51, bf16[2,512,384]{1,0,2:T(2,128)(2,1)S(1)} %copy-done.2, s32[]{:T(128)S(6)} %select_n.174, s32[]{:T(128)S(6)} %select_n.189, ...), kind=kLoop, calls=%fused_computation.27 | loop fusion | flops 786432 | bytes 3145748 | tf_op jit(solution)/shard_map/jit(_where)/select_n | solution.py:160
  117.8 2.9 %copy.387 = bf16[1,512,384]{2,1,0:T(8,128)(2,1)} copy(bf16[1,512,384]{1,0,2:T(2,128)(2,1)} %get-tuple-element.55) | data formatting | bytes 786432 | tf_op jit(solution)/shard_map/jit(_where)/select_n | solution.py:160
  122.7 2.9 %copy.389 = bf16[1,512,384]{2,1,0:T(8,128)(2,1)} copy(bf16[1,512,384]{1,0,2:T(2,128)(2,1)} %get-tuple-element.58) | data formatting | bytes 786432 | tf_op jit(solution)/shard_map/jit(_where)/select_n | solution.py:160
  125.6 5.2 %collective-permute-start.13 = (bf16[512,384]{1,0:T(8,128)(2,1)}, bf16[512,384]{1,0:T(8,128)(2,1)}, u32[]{:S(2)}, u32[]{:S(2)}) collective-permute-start(bf16[512,384]{1,0:T(8,128)(2,1)} %bitcast.129), channel_id=1, source_target_pairs={{4,0},{8,4},{12,8},{16,12},{20,16},{24,20},{28,24},{32,28},{36,32}... | collective-permute-start | bytes 1179656 | tf_op jit(solution)/shard_map/ppermute | solution.py:13
  132.5 6.9 %collective-permute-start.14 = (bf16[512,384]{1,0:T(8,128)(2,1)}, bf16[512,384]{1,0:T(8,128)(2,1)}, u32[]{:S(2)}, u32[]{:S(2)}) collective-permute-start(bf16[512,384]{1,0:T(8,128)(2,1)} %bitcast.128), channel_id=1, source_target_pairs={{0,4},{4,8},{8,12},{12,16},{16,20},{20,24},{24,28},{28,32},{32,36}... | collective-permute-start | bytes 1179656 | tf_op jit(solution)/shard_map/ppermute | solution.py:13
  145.1 4.2 %fusion.29 = f32[3,128,512]{2,1,0:T(8,128)} fusion(bf16[512,3,128]{0,2,1:T(8,128)(2,1)} %bitcast.133, f32[3,512,512]{1,2,0:T(8,128)} %get-tuple-element.66, f32[3,512]{1,0:T(4,128)S(1)} %add.115, f32[3,512]{1,0:T(4,128)S(1)} %max.13, pred[512,512]{0,1:T(8,128)(4,1)S(1)} %copy-done.17), kind=kOutput, calls=%fused_computation.48 | convolution fusion | flops 205258752 | bytes 4599808 | tf_op jit(solution)/shard_map/hqk,qhd->khd/dot_general | solution.py:134
  149.3 2.5 %multiply_convert_fusion.1 = bf16[3,512,512]{1,2,0:T(8,128)(2,1)} fusion(bf16[512,3,128]{0,2,1:T(8,128)(2,1)S(1)} %bitcast.135, bf16[512,3,128]{0,2,1:T(8,128)(2,1)S(1)} %bitcast.126, f32[3,512]{1,0:T(4,128)S(1)} %copy-done.25, f32[3,512]{1,0:T(4,128)S(1)} %add.115, f32[3,512]{1,0:T(4,128)S(1)} %max.13, f32[3,512,512]{1,2,0:T(8,128)S(1)} %copy-done.4, ...), kind=kOutput, calls=%fused_computation.8 | convolution fusion | flops 207618048 | bytes 5785600 | tf_op jit(solution)/shard_map/qhd,khd->hqk/dot_general | solution.py:113
  151.8 7.6 %broadcast_select_fusion.7 = (bf16[1,512,384]{1,0,2:T(2,128)(2,1)}, bf16[1,512,384]{1,0,2:T(2,128)(2,1)}, bf16[1,512,384]{1,0,2:T(2,128)(2,1)}, bf16[1,512,384]{1,0,2:T(2,128)(2,1)}) fusion(pred[]{:T(512)} %get-tuple-element.51, bf16[2,512,384]{1,0,2:T(2,128)(2,1)S(1)} %convert_element_type.84, s32[]{:T(128)S(6)} %select_n.174, s32[]{:T(128)S(6)} %select_n.189, ...), kind=kLoop, calls=%fused_computation.28 | loop fusion | flops 786432 | bytes 3145748 | tf_op jit(solution)/shard_map/jit(_where)/select_n | solution.py:159
  159.4 3.0 %copy.383 = bf16[1,512,384]{2,1,0:T(8,128)(2,1)} copy(bf16[1,512,384]{1,0,2:T(2,128)(2,1)} %get-tuple-element.61) | data formatting | bytes 786432 | tf_op jit(solution)/shard_map/jit(_where)/select_n | solution.py:159
  162.4 2.3 %collective-permute-start.10 = (bf16[512,384]{1,0:T(8,128)(2,1)}, bf16[512,384]{1,0:T(8,128)(2,1)}, u32[]{:S(2)}, u32[]{:S(2)}) collective-permute-start(bf16[512,384]{1,0:T(8,128)(2,1)} %bitcast.130), channel_id=1, source_target_pairs={{0,4},{4,8},{8,12},{12,16},{16,20},{20,24},{24,28},{28,32},{32,36}... | collective-permute-start | bytes 1179656 | tf_op jit(solution)/shard_map/ppermute | solution.py:13
  164.7 2.5 %fusion.27 = bf16[512,3,128]{0,2,1:T(8,128)(2,1)} fusion(f32[512,3,128]{0,2,1:T(8,128)S(1)} %copy-done.11, bf16[512,3,128]{0,2,1:T(8,128)(2,1)S(1)} %bitcast.117, bf16[3,512,512]{1,2,0:T(8,128)(2,1)} %multiply_convert_fusion.1), kind=kOutput, calls=%fused_computation.40 | convolution fusion | flops 201719808 | bytes 3145728 | tf_op jit(solution)/shard_map/hqk,khd->qhd/dot_general | solution.py:123
  167.2 2.9 %copy.384 = bf16[1,512,384]{2,1,0:T(8,128)(2,1)} copy(bf16[1,512,384]{1,0,2:T(2,128)(2,1)} %get-tuple-element.60) | data formatting | bytes 786432 | tf_op jit(solution)/shard_map/jit(_where)/select_n | solution.py:159
  170.1 2.9 %copy.380 = bf16[1,512,384]{2,1,0:T(8,128)(2,1)} copy(bf16[1,512,384]{1,0,2:T(2,128)(2,1)} %get-tuple-element.59) | data formatting | bytes 786432 | tf_op jit(solution)/shard_map/jit(_where)/select_n | solution.py:159
  176.6 3.6 %collective-permute-start.8 = (bf16[512,384]{1,0:T(8,128)(2,1)}, bf16[512,384]{1,0:T(8,128)(2,1)}, u32[]{:S(2)}, u32[]{:S(2)}) collective-permute-start(bf16[512,384]{1,0:T(8,128)(2,1)} %bitcast.27), channel_id=1, source_target_pairs={{8,0},{12,4},{16,8},{20,12},{24,16},{28,20},{32,24},{36,28},{40,32... | collective-permute-start | bytes 1179656 | tf_op jit(solution)/shard_map/ppermute | solution.py:13
  180.3 2.6 %collective-permute-start.9 = (bf16[512,384]{1,0:T(8,128)(2,1)}, bf16[512,384]{1,0:T(8,128)(2,1)}, u32[]{:S(2)}, u32[]{:S(2)}) collective-permute-start(bf16[512,384]{1,0:T(8,128)(2,1)} %bitcast.28), channel_id=1, source_target_pairs={{4,0},{8,4},{12,8},{16,12},{20,16},{24,20},{28,24},{32,28},{36,32}... | collective-permute-start | bytes 1179656 | tf_op jit(solution)/shard_map/ppermute | solution.py:13
  188.5 2.3 %add_convert_fusion = bf16[512,384]{1,0:T(8,128)(2,1)} fusion(bf16[512,384]{1,0:T(8,128)(2,1)} %collective-permute-done.15, bf16[512,384]{1,0:T(8,128)(2,1)} %collective-permute-done.14, bf16[512,384]{1,0:T(8,128)(2,1)} %collective-permute-done.13, f32[512,384]{1,0:T(8,128)S(1)} %copy.388, bf16[512,384]{1,0:T(8,128)(2,1)} %collective-permute-done.12), kind=kLoop, calls=%fused_computation.46 | loop fusion | flops 1769472 | bytes 2752512 | tf_op jit(solution)/shard_map/convert_element_type | solution.py:165
  192.4 4.8 %collective-permute-done.9 = bf16[512,384]{1,0:T(8,128)(2,1)} collective-permute-done((bf16[512,384]{1,0:T(8,128)(2,1)}, bf16[512,384]{1,0:T(8,128)(2,1)}, u32[]{:S(2)}, u32[]{:S(2)}) %collective-permute-start.9) | collective-permute-done | bytes 393248 | tf_op jit(solution)/shard_map/ppermute | solution.py:13
  197.2 2.3 %add_convert_fusion.1 = bf16[512,384]{1,0:T(8,128)(2,1)} fusion(bf16[512,384]{1,0:T(8,128)(2,1)} %collective-permute-done.11, bf16[512,384]{1,0:T(8,128)(2,1)} %collective-permute-done.10, bf16[512,384]{1,0:T(8,128)(2,1)} %collective-permute-done.9, f32[512,384]{1,0:T(8,128)S(1)} %copy.381, bf16[512,384]{1,0:T(8,128)(2,1)} %collective-permute-done.8), kind=kLoop, calls=%fused_computation.47 | loop fusion | flops 1769472 | bytes 2752512 | tf_op jit(solution)/shard_map/convert_element_type | solution.py:164
  (119 shorter events, 63.8 us)
Async XLA Ops:
  7.2 77.2 %copy-start = (bf16[384,1536]{1,0:T(8,128)(2,1)S(1)}, bf16[384,1536]{1,0:T(8,128)(2,1)}, u32[]{:S(2)}) copy-start(bf16[384,1536]{1,0:T(8,128)(2,1)} %param.12) | copy-start | bytes 3538948
  7.2 77.2 %all-gather.2.cloned.1.call-start = ((), (), s32[]{:S(2)}) async-start(), calls=%async_computation.1 | async-start | bytes 1966080 | tf_op jit(solution)/shard_map/all_gather | solution.py:50
  7.2 35.4 %collective-permute-start = (bf16[512,384]{1,0:T(8,128)(2,1)}, bf16[512,384]{1,0:T(8,128)(2,1)S(1)}, u32[]{:S(2)}, u32[]{:S(2)}) collective-permute-start(bf16[512,384]{1,0:T(8,128)(2,1)} %param.10), channel_id=1, source_target_pairs={{0,8},{4,12},{8,16},{12,20},{16,24},{20,28},{24,32},{28,36},{32,40... | collective-permute-start | bytes 1179656 | tf_op jit(solution)/shard_map/ppermute | solution.py:13
  12.0 34.8 %collective-permute-start.1 = (bf16[512,384]{1,0:T(8,128)(2,1)}, bf16[512,384]{1,0:T(8,128)(2,1)S(1)}, u32[]{:S(2)}, u32[]{:S(2)}) collective-permute-start(bf16[512,384]{1,0:T(8,128)(2,1)} %param.10), channel_id=1, source_target_pairs={{0,4},{4,8},{8,12},{12,16},{16,20},{20,24},{24,28},{28,32},{32,36}... | collective-permute-start | bytes 1179656 | tf_op jit(solution)/shard_map/ppermute | solution.py:13
  16.0 32.7 %collective-permute-start.2 = (bf16[512,384]{1,0:T(8,128)(2,1)}, bf16[512,384]{1,0:T(8,128)(2,1)}, u32[]{:S(2)}, u32[]{:S(2)}) collective-permute-start(bf16[512,384]{1,0:T(8,128)(2,1)} %param.10), channel_id=1, source_target_pairs={{4,0},{8,4},{12,8},{16,12},{20,16},{24,20},{28,24},{32,28},{36,32}... | collective-permute-start | bytes 1179656 | tf_op jit(solution)/shard_map/ppermute | solution.py:13
  17.9 35.5 %collective-permute-start.3 = (bf16[512,384]{1,0:T(8,128)(2,1)}, bf16[512,384]{1,0:T(8,128)(2,1)}, u32[]{:S(2)}, u32[]{:S(2)}) collective-permute-start(bf16[512,384]{1,0:T(8,128)(2,1)} %param.10), channel_id=1, source_target_pairs={{8,0},{12,4},{16,8},{20,12},{24,16},{28,20},{32,24},{36,28},{40,32... | collective-permute-start | bytes 1179656 | tf_op jit(solution)/shard_map/ppermute | solution.py:13
  20.1 38.0 %collective-permute-start.4 = (bf16[512,384]{1,0:T(8,128)(2,1)}, bf16[512,384]{1,0:T(8,128)(2,1)S(1)}, u32[]{:S(2)}, u32[]{:S(2)}) collective-permute-start(bf16[512,384]{1,0:T(8,128)(2,1)} %param.11), channel_id=1, source_target_pairs={{0,8},{4,12},{8,16},{12,20},{16,24},{20,28},{24,32},{28,36},{32,40... | collective-permute-start | bytes 1179656 | tf_op jit(solution)/shard_map/ppermute | solution.py:13
  26.6 173.0 %reduce-scatter.4.cloned.1.call-start = ((), (), s32[]{:S(2)}) async-start(), calls=%async_computation.2 | async-start | bytes 1966080
  30.9 25.1 %copy-start.12 = (bf16[512,384]{0,1:T(8,128)(2,1)}, bf16[512,384]{0,1:T(8,128)(2,1)S(1)}, u32[]{:S(2)}) copy-start(bf16[512,384]{0,1:T(8,128)(2,1)S(1)} %copy.359) | copy-start | bytes 1179652
  39.1 39.4 %copy-start.7 = (bf16[512,384]{0,1:T(8,128)(2,1)}, bf16[512,384]{0,1:T(8,128)(2,1)S(1)}, u32[]{:S(2)}) copy-start(bf16[512,384]{0,1:T(8,128)(2,1)S(1)} %copy.358) | copy-start | bytes 1179652
  42.6 39.6 %copy-start.16 = (pred[512,512]{0,1:T(8,128)(4,1)}, pred[512,512]{0,1:T(8,128)(4,1)S(1)}, u32[]{:S(2)}) copy-start(pred[512,512]{0,1:T(8,128)(4,1)S(1)} %broadcast_compare_fusion) | copy-start | bytes 786436
  42.6 15.5 %collective-permute-start.5 = (bf16[512,384]{1,0:T(8,128)(2,1)}, bf16[512,384]{1,0:T(8,128)(2,1)}, u32[]{:S(2)}, u32[]{:S(2)}) collective-permute-start(bf16[512,384]{1,0:T(8,128)(2,1)} %param.11), channel_id=1, source_target_pairs={{0,4},{4,8},{8,12},{12,16},{16,20},{20,24},{24,28},{28,32},{32,36}... | collective-permute-start | bytes 1179656 | tf_op jit(solution)/shard_map/ppermute | solution.py:13
  46.8 15.6 %collective-permute-start.6 = (bf16[512,384]{1,0:T(8,128)(2,1)}, bf16[512,384]{1,0:T(8,128)(2,1)}, u32[]{:S(2)}, u32[]{:S(2)}) collective-permute-start(bf16[512,384]{1,0:T(8,128)(2,1)} %param.11), channel_id=1, source_target_pairs={{4,0},{8,4},{12,8},{16,12},{20,16},{24,20},{28,24},{32,28},{36,32}... | collective-permute-start | bytes 1179656 | tf_op jit(solution)/shard_map/ppermute | solution.py:13
  48.8 16.7 %collective-permute-start.7 = (bf16[512,384]{1,0:T(8,128)(2,1)}, bf16[512,384]{1,0:T(8,128)(2,1)}, u32[]{:S(2)}, u32[]{:S(2)}) collective-permute-start(bf16[512,384]{1,0:T(8,128)(2,1)} %param.11), channel_id=1, source_target_pairs={{8,0},{12,4},{16,8},{20,12},{24,16},{28,20},{32,24},{36,28},{40,32... | collective-permute-start | bytes 1179656 | tf_op jit(solution)/shard_map/ppermute | solution.py:13
  74.5 5.0 %copy-start.5 = (bf16[1024,3,128]{0,2,1:T(8,128)(2,1)}, bf16[1024,3,128]{0,2,1:T(8,128)(2,1)S(1)}, u32[]{:S(2)}) copy-start(bf16[1024,3,128]{0,2,1:T(8,128)(2,1)S(1)} %reshape_squeeze.6) | copy-start | bytes 2359300
  92.5 8.3 %slice-start = ((s8[6291456]{0:T(1024)(128)(4,1)}), s8[2097152]{0:T(1024)(128)(4,1)S(1)}, s32[]{:S(2)}) async-start(s8[6291456]{0:T(1024)(128)(4,1)} %bitcast.109), calls=%async_computation.3 | async-start | bytes 4194304
  95.9 4.9 %copy-start.22 = (bf16[512,384]{0,1:T(8,128)(2,1)S(1)}, bf16[512,384]{0,1:T(8,128)(2,1)}, u32[]{:S(2)}) copy-start(bf16[512,384]{0,1:T(8,128)(2,1)} %copy-done.21) | copy-start | bytes 1179652
  108.0 7.9 %copy-start.8 = (bf16[512,384]{0,1:T(8,128)(2,1)S(1)}, bf16[512,384]{0,1:T(8,128)(2,1)}, u32[]{:S(2)}) copy-start(bf16[512,384]{0,1:T(8,128)(2,1)} %copy-done.7) | copy-start | bytes 1179652
  108.0 7.9 %copy-start.10 = (bf16[3,512,1024]{1,2,0:T(8,128)(2,1)S(1)}, bf16[3,512,1024]{1,2,0:T(8,128)(2,1)}, u32[]{:S(2)}) copy-start(bf16[3,512,1024]{1,2,0:T(8,128)(2,1)} %copy-done.9) | copy-start | bytes 9437188
  115.9 14.9 %copy-start.15 = (bf16[1,512,384]{1,0,2:T(2,128)(2,1)S(1)}, bf16[1,512,384]{1,0,2:T(2,128)(2,1)}, u32[]{:S(2)}) copy-start(bf16[1,512,384]{1,0,2:T(2,128)(2,1)} %get-tuple-element.57) | copy-start | bytes 1179652
  120.7 54.0 %collective-permute-start.12 = (bf16[512,384]{1,0:T(8,128)(2,1)}, bf16[512,384]{1,0:T(8,128)(2,1)}, u32[]{:S(2)}, u32[]{:S(2)}) collective-permute-start(bf16[512,384]{1,0:T(8,128)(2,1)} %bitcast.34), channel_id=1, source_target_pairs={{8,0},{12,4},{16,8},{20,12},{24,16},{28,20},{32,24},{36,28},{40,32... | collective-permute-start | bytes 1179656 | tf_op jit(solution)/shard_map/ppermute | solution.py:13
  122.6 22.4 %copy-start.17 = (pred[512,512]{0,1:T(8,128)(4,1)S(1)}, pred[512,512]{0,1:T(8,128)(4,1)}, u32[]{:S(2)}) copy-start(pred[512,512]{0,1:T(8,128)(4,1)} %copy-done.16) | copy-start | bytes 786436
  125.6 51.0 %collective-permute-start.13 = (bf16[512,384]{1,0:T(8,128)(2,1)}, bf16[512,384]{1,0:T(8,128)(2,1)}, u32[]{:S(2)}, u32[]{:S(2)}) collective-permute-start(bf16[512,384]{1,0:T(8,128)(2,1)} %bitcast.129), channel_id=1, source_target_pairs={{4,0},{8,4},{12,8},{16,12},{20,16},{24,20},{28,24},{32,28},{36,32}... | collective-permute-start | bytes 1179656 | tf_op jit(solution)/shard_map/ppermute | solution.py:13
  132.5 47.8 %collective-permute-start.14 = (bf16[512,384]{1,0:T(8,128)(2,1)}, bf16[512,384]{1,0:T(8,128)(2,1)}, u32[]{:S(2)}, u32[]{:S(2)}) collective-permute-start(bf16[512,384]{1,0:T(8,128)(2,1)} %bitcast.128), channel_id=1, source_target_pairs={{0,4},{4,8},{8,12},{12,16},{16,20},{20,24},{24,28},{28,32},{32,36}... | collective-permute-start | bytes 1179656 | tf_op jit(solution)/shard_map/ppermute | solution.py:13
  141.0 47.5 %collective-permute-start.15 = (bf16[512,384]{1,0:T(8,128)(2,1)}, bf16[512,384]{1,0:T(8,128)(2,1)}, u32[]{:S(2)}, u32[]{:S(2)}) collective-permute-start(bf16[512,384]{1,0:T(8,128)(2,1)} %bitcast.37), channel_id=1, source_target_pairs={{0,8},{4,12},{8,16},{12,20},{16,24},{20,28},{24,32},{28,36},{32,40... | collective-permute-start | bytes 1179656 | tf_op jit(solution)/shard_map/ppermute | solution.py:13
  151.8 12.9 %copy-start.11 = (f32[512,3,128]{0,2,1:T(8,128)S(1)}, f32[512,3,128]{0,2,1:T(8,128)}, u32[]{:S(2)}) copy-start(f32[512,3,128]{0,2,1:T(8,128)} %convolution_bitcast_fusion.2) | copy-start | bytes 2359300
  151.8 12.9 %copy-start.13 = (bf16[512,384]{0,1:T(8,128)(2,1)S(1)}, bf16[512,384]{0,1:T(8,128)(2,1)}, u32[]{:S(2)}) copy-start(bf16[512,384]{0,1:T(8,128)(2,1)} %copy-done.12) | copy-start | bytes 1179652
  159.4 13.6 %copy-start.14 = (bf16[1,512,384]{1,0,2:T(2,128)(2,1)S(1)}, bf16[1,512,384]{1,0,2:T(2,128)(2,1)}, u32[]{:S(2)}) copy-start(bf16[1,512,384]{1,0,2:T(2,128)(2,1)} %get-tuple-element.62) | copy-start | bytes 1179652
  162.4 28.5 %collective-permute-start.10 = (bf16[512,384]{1,0:T(8,128)(2,1)}, bf16[512,384]{1,0:T(8,128)(2,1)}, u32[]{:S(2)}, u32[]{:S(2)}) collective-permute-start(bf16[512,384]{1,0:T(8,128)(2,1)} %bitcast.130), channel_id=1, source_target_pairs={{0,4},{4,8},{8,12},{12,16},{16,20},{20,24},{24,28},{28,32},{32,36}... | collective-permute-start | bytes 1179656 | tf_op jit(solution)/shard_map/ppermute | solution.py:13
  174.7 16.2 %collective-permute-start.11 = (bf16[512,384]{1,0:T(8,128)(2,1)}, bf16[512,384]{1,0:T(8,128)(2,1)}, u32[]{:S(2)}, u32[]{:S(2)}) collective-permute-start(bf16[512,384]{1,0:T(8,128)(2,1)} %bitcast.30), channel_id=1, source_target_pairs={{0,8},{4,12},{8,16},{12,20},{16,24},{20,28},{24,32},{28,36},{32,40... | collective-permute-start | bytes 1179656 | tf_op jit(solution)/shard_map/ppermute | solution.py:13
  176.6 15.8 %collective-permute-start.8 = (bf16[512,384]{1,0:T(8,128)(2,1)}, bf16[512,384]{1,0:T(8,128)(2,1)}, u32[]{:S(2)}, u32[]{:S(2)}) collective-permute-start(bf16[512,384]{1,0:T(8,128)(2,1)} %bitcast.27), channel_id=1, source_target_pairs={{8,0},{12,4},{16,8},{20,12},{24,16},{28,20},{32,24},{36,28},{40,32... | collective-permute-start | bytes 1179656 | tf_op jit(solution)/shard_map/ppermute | solution.py:13
  180.3 16.9 %collective-permute-start.9 = (bf16[512,384]{1,0:T(8,128)(2,1)}, bf16[512,384]{1,0:T(8,128)(2,1)}, u32[]{:S(2)}, u32[]{:S(2)}) collective-permute-start(bf16[512,384]{1,0:T(8,128)(2,1)} %bitcast.28), channel_id=1, source_target_pairs={{4,0},{8,4},{12,8},{16,12},{20,16},{24,20},{28,24},{32,28},{36,32}... | collective-permute-start | bytes 1179656 | tf_op jit(solution)/shard_map/ppermute | solution.py:13
  (14 other events, 42.0 us)
Sparse Core Ops, SparseCore 0:
  26.7 27.0 all-gather.1
  108.1 28.1 reduce-scatter.3
where the time goes:
time: 210 us; the launch traced here: 208 us
  starting transfers between devices  54.1 us (26%)
  local copies, waits for them, and re-layouts  49.3 us (23%)
  matrix products  36.5 us (17%)
  other arithmetic  32.5 us (15%)
  between operations  22.2 us (11%)
  waiting for transfers between devices  13.8 us (7%)
    ppermute x16, starting transfers between devices, shifted(): return lax.ppermute(block, axis, route)  54 us
    ppermute x16, waiting for transfers between devices, shifted(): return lax.ppermute(block, axis, route)  13.7 us
    unnamed x62, local copies, waits for them, and re-layouts  11.6 us
    select_n x4, local copies, waits for them, and re-layouts, on_device(): part_keys = jnp.where(any_match, sent_keys[slot_index], zero_tile)  10.4 us
    select_n x4, local copies, waits for them, and re-layouts, on_device(): part_values = jnp.where(any_match, sent_values[slot_index], zero_tile)  9.19 us
    select_n x1, other arithmetic, on_device(): part_values = jnp.where(any_match, sent_values[slot_index], zero_tile)  7.85 us
    select_n x1, other arithmetic, on_device(): part_keys = jnp.where(any_match, sent_keys[slot_index], zero_tile)  7.63 us
    dot_general x1, matrix products, on_device(): jnp.einsum('hqk,qhd->khd', low_route, grad_rows, preferred_element_type=j...  5.22 us
  transfers between devices with their start and end apart: 18, of which 4 were waited for; matrix products, arithmetic and copies ran while one was open for 44% of the time, Pallas kernels for 0%

commit v1 on v0

v1 whole, which is shorter than its diff:
```python
import functools

import jax
import jax.numpy as jnp
from jax import lax
from jax.experimental import pallas as pl
from jax.experimental.pallas import tpu as pltpu
from jax.sharding import PartitionSpec as P

HEAD_DIM = 128
BLOCK_LEN = 512
NEG_BIG = -1e30
INTERPRET = None


def shifted(block, axis, distance):
    devices = range(lax.axis_size(axis))
    route = [(i - distance, i) for i in devices if i - distance in devices]
    return lax.ppermute(block, axis, route)


def partner_swap(block, axis):
    size = lax.axis_size(axis)
    return lax.ppermute(block, axis, [(i, i ^ 1) for i in range(size)])


def pack_heads(keys, values):
    rows, columns = keys.shape
    heads = columns // HEAD_DIM
    k4 = keys.reshape(rows, heads, 1, HEAD_DIM)
    v4 = values.reshape(rows, heads, 1, HEAD_DIM)
    return jnp.concatenate([k4, v4], axis=2).reshape(rows, 2 * columns)


def unpack_heads(packed):
    rows, wide = packed.shape
    heads = wide // (2 * HEAD_DIM)
    p4 = packed.reshape(rows, heads, 2, HEAD_DIM)
    return (p4[:, :, 0, :].reshape(rows, heads * HEAD_DIM), p4[:, :, 1, :].reshape(rows, heads * HEAD_DIM))


def attn_kernel(sel_ref, q_ref, kv0_ref, c0_ref, c1_ref, c2_ref, c3_ref, g_ref, srow_ref, scol_ref,
                attn_ref, dq_ref, dkv0_ref, dkv1_ref, dkv2_ref):
    scale = HEAD_DIM ** (-0.5)
    d = HEAD_DIM
    cands = (c0_ref, c1_ref, c2_ref, c3_ref)

    def pick(slot):
        idx = sel_ref[slot]
        out = cands[0][...]
        for c in range(1, 4):
            out = jnp.where(idx == c, cands[c][...], out)
        return out

    kv = [kv0_ref[...], pick(0), pick(1)]
    ks = [x[:, :d] for x in kv]
    vs = [x[:, d:] for x in kv]
    q = q_ref[...]
    g = g_ref[...]
    nt = (((1,), (1,)), ((), ()))
    tn = (((0,), (0,)), ((), ()))
    scores = [lax.dot_general(q, k, nt, preferred_element_type=jnp.float32) * scale for k in ks]
    visible = srow_ref[...] == scol_ref[...]
    scores[0] = jnp.where(visible, scores[0], NEG_BIG)
    top = jnp.max(scores[0], axis=1, keepdims=True)
    for s in scores[1:]:
        top = jnp.maximum(top, jnp.max(s, axis=1, keepdims=True))
    weights = [jnp.exp(s - top) for s in scores]
    weights[0] = jnp.where(visible, weights[0], 0.0)
    total = weights[0].sum(axis=1, keepdims=True)
    for w in weights[1:]:
        total = total + w.sum(axis=1, keepdims=True)
    inv = 1.0 / total
    probs = [w * inv for w in weights]
    low = [p.astype(jnp.bfloat16) for p in probs]
    acc = jnp.dot(low[0], vs[0], preferred_element_type=jnp.float32)
    for j in (1, 2):
        acc = acc + jnp.dot(low[j], vs[j], preferred_element_type=jnp.float32)
    attn = acc.astype(jnp.bfloat16)
    attn_ref[...] = attn
    gf = g.astype(jnp.float32)
    delta = jnp.sum(attn.astype(jnp.float32) * gf, axis=1, keepdims=True)
    dq = None
    outs = (dkv0_ref, dkv1_ref, dkv2_ref)
    for j in range(3):
        dp = lax.dot_general(g, vs[j], nt, preferred_element_type=jnp.float32)
        ds = (probs[j] * (dp - delta) * scale).astype(jnp.bfloat16)
        part = jnp.dot(ds, ks[j], preferred_element_type=jnp.float32)
        dq = part if dq is None else dq + part
        dk = lax.dot_general(ds, q, tn, preferred_element_type=jnp.float32)
        dv = lax.dot_general(low[j], g, tn, preferred_element_type=jnp.float32)
        outs[j][:, :d] = dk.astype(outs[j].dtype)
        outs[j][:, d:] = dv.astype(outs[j].dtype)
    dq_ref[...] = dq.astype(jnp.bfloat16)


def attention(sel, queries, kv_self, cands, grad_attn, shot_ids):
    rows, columns = queries.shape
    heads = columns // HEAD_DIM
    d = HEAD_DIM
    col = lambda h, s: (0, h)
    spec_q = pl.BlockSpec((rows, d), col)
    spec_kv = pl.BlockSpec((rows, 2 * d), col)
    grid_spec = pltpu.PrefetchScalarGridSpec(
        num_scalar_prefetch=1,
        grid=(heads,),
        in_specs=[spec_q, spec_kv, spec_kv, spec_kv, spec_kv, spec_kv, spec_q,
                  pl.BlockSpec((rows, 1), lambda h, s: (0, 0)),
                  pl.BlockSpec((1, rows), lambda h, s: (0, 0))],
        out_specs=[spec_q, spec_q, spec_kv, spec_kv, spec_kv],
    )
    out_shape = [
        jax.ShapeDtypeStruct((rows, columns), jnp.bfloat16),
        jax.ShapeDtypeStruct((rows, columns), jnp.bfloat16),
        jax.ShapeDtypeStruct((rows, 2 * columns), jnp.float32),
        jax.ShapeDtypeStruct((rows, 2 * columns), jnp.bfloat16),
        jax.ShapeDtypeStruct((rows, 2 * columns), jnp.bfloat16),
    ]
    kwargs = {}
    if INTERPRET is not None:
        kwargs["interpret"] = INTERPRET
    return pl.pallas_call(
        attn_kernel,
        grid_spec=grid_spec,
        out_shape=out_shape,
        compiler_params=pltpu.CompilerParams(vmem_limit_bytes=48 * 1024 * 1024),
        **kwargs,
    )(sel, queries, kv_self, *cands, grad_attn, shot_ids.reshape(rows, 1), shot_ids.reshape(1, rows))


def on_device(queries, keys, values, out_weight, cotangent, routes, shot_ids):
    seq_index = lax.axis_index("seq")
    tok_rows, columns = queries.shape
    parity = seq_index % 2
    cot_full = lax.all_gather(cotangent, "head", axis=1, tiled=True)
    grad_attn = lax.dot_general(
        cot_full, out_weight, (((1,), (1,)), ((), ())), preferred_element_type=jnp.float32
    ).astype(jnp.bfloat16)
    own_kv = pack_heads(keys, values)
    from_left2 = shifted(own_kv, "seq", 2)
    from_right2 = shifted(own_kv, "seq", -2)
    partner_own = partner_swap(own_kv, "seq")
    relay_out = jnp.where(parity == 0, from_right2, from_left2)
    partner_relay = partner_swap(relay_out, "seq")
    partner_off = 1 - 2 * parity
    offs = routes[seq_index] - seq_index
    sel = jnp.where(offs == -2, 0, jnp.where(offs == 2, 3, jnp.where(offs == partner_off, 1, 2)))
    sel = sel.astype(jnp.int32)
    cands = (from_left2, partner_own, partner_relay, from_right2)
    attn, grad_q, self_term, term1, term2 = attention(sel, queries, own_kv, cands, grad_attn, shot_ids)
    partial_out = jnp.dot(attn, out_weight, preferred_element_type=jnp.float32)
    attn_out = lax.psum_scatter(partial_out.astype(jnp.bfloat16), "head", scatter_dimension=1, tiled=True)
    zero = jnp.zeros_like(term1)

    def term_for(offset):
        return jnp.where(offs[0] == offset, term1, jnp.where(offs[1] == offset, term2, zero))

    t_plus1 = term_for(1)
    t_minus1 = term_for(-1)
    to_partner_own = jnp.where(parity == 0, t_plus1, t_minus1)
    to_partner_relay = jnp.where(parity == 0, t_minus1, t_plus1)
    back_own = partner_swap(to_partner_own, "seq")
    back_relay = partner_swap(to_partner_relay, "seq").astype(jnp.float32)
    up_plus = term_for(2).astype(jnp.float32) + jnp.where(parity == 0, back_relay, 0.0)
    up_minus = term_for(-2).astype(jnp.float32) + jnp.where(parity == 1, back_relay, 0.0)
    got_from_left = shifted(up_plus.astype(jnp.bfloat16), "seq", 2)
    got_from_right = shifted(up_minus.astype(jnp.bfloat16), "seq", -2)
    total = (
        self_term
        + back_own.astype(jnp.float32)
        + got_from_left.astype(jnp.float32)
        + got_from_right.astype(jnp.float32)
    )
    grad_keys, grad_values = unpack_heads(total.astype(jnp.bfloat16))
    return (attn_out, grad_q, grad_keys, grad_values)


def solution(mesh):
    in_specs = (
        P("seq", "head"),
        P("seq", "head"),
        P("seq", "head"),
        P("head", None),
        P("seq", "head"),
        P(),
        P("seq"),
    )
    out_specs = (P("seq", "head"), P("seq", "head"), P("seq", "head"), P("seq", "head"))
    return jax.shard_map(
        on_device, mesh=mesh, in_specs=in_specs, out_specs=out_specs, check_vma=False
    )
```

time: 210 us -> 119 us (0.57)
  the two profiles are of different devices: /device:TPU:111 before, /device:TPU:126 now
where the time goes in v1:
time: 119 us
  waiting for transfers between devices  44 us (37%)
  between operations  19.5 us (16%)
  local copies, waits for them, and re-layouts  16.7 us (14%)
  Pallas kernels  15.6 us (13%)
  starting transfers between devices  13.7 us (12%)
  other arithmetic  5.64 us (5%)
  matrix products  3.43 us (3%)
    ppermute x4, waiting for transfers between devices, shifted(): return lax.ppermute(block, axis, route)  43.3 us
    pallas_call x1, Pallas kernels, attention(): pl.pallas_call(attn_kernel, grid_spec=grid_spec, out_shape=out_shape, com...  15.6 us
    ppermute x4, starting transfers between devices, shifted(): return lax.ppermute(block, axis, route)  12.9 us
    unnamed x28, local copies, waits for them, and re-layouts  12.6 us
    dot_general x1, matrix products, on_device(): lax.dot_general(cot_full, out_weight, (((1,), (1,)), ((), ())), preferred...  2.46 us
  transfers between devices with their start and end apart: 10, of which 4 were waited for; matrix products, arithmetic and copies ran while one was open for 16% of the time, Pallas kernels for 0%

profile of v1, /device:TPU:126, one launch (start us, length us, event | category | flops | bytes accessed | tf_op | source)
XLA Modules:
  0.0 118.6 jit_solution(16120986342304725821)
XLA Ops:
  7.2 0.7 all-gather.2.cloned.1.call-update
  8.0 1.2 copy.21
  9.1 1.2 copy.22
  10.4 1.1 copy.23
  11.5 0.4 reshape.83.kv0_ref
  11.9 5.0 %collective-permute-start = (bf16[512,768]{1,0:T(8,128)(2,1)S(1)}, bf16[512,768]{1,0:T(8,128)(2,1)S(1)}, u32[]{:S(2)}, u32[]{:S(2)}) collective-permute-start(bf16[512,768]{1,0:T(8,128)(2,1)S(1)} %reshape.83.kv0_ref), channel_id=1, source_target_pairs={{0,8},{4,12},{8,16},{12,20},{16,24},{20,28},{24,32},{28,36},{32,40... | collective-permute-start | bytes 2359304 | tf_op jit(solution)/shard_map/ppermute | solution.py:19
  16.9 1.9 %collective-permute-start.2 = (bf16[512,768]{1,0:T(8,128)(2,1)S(1)}, bf16[512,768]{1,0:T(8,128)(2,1)}, u32[]{:S(2)}, u32[]{:S(2)}) collective-permute-start(bf16[512,768]{1,0:T(8,128)(2,1)S(1)} %reshape.83.kv0_ref), channel_id=1, source_target_pairs={{8,0},{12,4},{16,8},{20,12},{24,16},{28,20},{32,24},{36,28},{40,32... | collective-permute-start | bytes 2359304 | tf_op jit(solution)/shard_map/ppermute | solution.py:19
  18.9 14.7 %collective-permute-done.c0_ref = bf16[512,768]{1,0:T(8,128)(2,1)S(1)} collective-permute-done((bf16[512,768]{1,0:T(8,128)(2,1)S(1)}, bf16[512,768]{1,0:T(8,128)(2,1)S(1)}, u32[]{:S(2)}, u32[]{:S(2)}) %collective-permute-start) | collective-permute-done | bytes 786464 | tf_op jit(solution)/shard_map/ppermute | solution.py:19
  33.7 7.5 %collective-permute-done.2.c3_ref = bf16[512,768]{1,0:T(8,128)(2,1)} collective-permute-done((bf16[512,768]{1,0:T(8,128)(2,1)S(1)}, bf16[512,768]{1,0:T(8,128)(2,1)}, u32[]{:S(2)}, u32[]{:S(2)}) %collective-permute-start.2) | collective-permute-done | bytes 786464 | tf_op jit(solution)/shard_map/ppermute | solution.py:19
  41.2 2.1 %broadcast_select_fusion.2 = bf16[512,768]{1,0:T(8,128)(2,1)} fusion(bf16[512,768]{1,0:T(8,128)(2,1)} %collective-permute-done.2.c3_ref, bf16[512,768]{1,0:T(8,128)(2,1)S(1)} %collective-permute-done.c0_ref, pred[]{:T(512)S(6)} %eq.89), kind=kLoop, calls=%fused_computation.14 | loop fusion | flops 393216 | bytes 2359297 | tf_op jit(solution)/shard_map/jit(_where)/select_n | solution.py:143
  43.3 0.9 copy.24.srow_ref
  44.4 2.5 %convolution_convert_fusion.1.g_ref = bf16[512,384]{1,0:T(8,128)(2,1)S(1)} fusion(bf16[512,1536]{1,0:T(8,128)(2,1)} %all-gather.2.cloned.1.call-done, bf16[384,1536]{1,0:T(8,128)(2,1)S(1)} %copy-done), kind=kOutput, calls=%fused_computation.8 | convolution fusion | flops 604176384 | bytes 3145728 | tf_op jit(solution)/shard_map/dot_general | solution.py:136
  46.9 0.9 copy-done.4
  47.8 1.1 copy-done.5
  48.9 15.6 %shard_map.102 = (bf16[512,384]{1,0:T(8,128)(2,1)S(1)}, bf16[512,384]{1,0:T(8,128)(2,1)}, f32[512,768]{1,0:T(8,128)}, bf16[512,768]{1,0:T(8,128)(2,1)S(1)}, bf16[512,768]{1,0:T(8,128)(2,1)S(1)}) custom-call(s32[2]{0:T(128)S(1)} %get-tuple-element.22.sel_ref, bf16[512,384]{1,0:T(8,128)(2,1)S(1)} %copy-done.6, bf16[512,768]{1,0:T(8,128)(2,1)S(1)} %reshape.83.kv0_ref, ...), custom_call_target="tpu_custom_call" | custom-call | tf_op jit(solution)/shard_map/pallas_call | solution.py:122
  64.5 0.9 copy-done.1
  65.4 1.0 convolution_convert_fusion
  66.4 1.6 %copy.29 = bf16[512,1536]{0,1:T(8,128)(2,1)} copy(bf16[512,1536]{1,0:T(8,128)(2,1)S(1)} %convolution_convert_fusion) | data formatting | bytes 3145728
  68.0 0.5 fusion.6
  71.1 1.0 broadcast_select_fusion.1
  72.2 0.5 collective-permute-start.5
  75.4 1.9 %fusion.1 = (bf16[512,768]{1,0:T(8,128)(2,1)S(1)}, bf16[512,768]{1,0:T(8,128)(2,1)S(1)}) fusion(bf16[512,768]{1,0:T(8,128)(2,1)} %collective-permute-done.5, bf16[512,768]{1,0:T(8,128)(2,1)S(1)} %get-tuple-element.12, bf16[512,768]{1,0:T(8,128)(2,1)S(1)} %copy-done.2, pred[]{:T(512)} %bitcast.9, pred[]{:T(512)} %bitcast.8, pred[]{:T(512)S(6)} %eq.89, ...), kind=kLoop, calls=%fused_computation.4 | loop fusion | flops 5111808 | bytes 3932166 | tf_op jit(solution)/shard_map/convert_element_type | solution.py:166
  77.3 1.9 %collective-permute-start.6 = (bf16[512,768]{1,0:T(8,128)(2,1)S(1)}, bf16[512,768]{1,0:T(8,128)(2,1)S(1)}, u32[]{:S(2)}, u32[]{:S(2)}) collective-permute-start(bf16[512,768]{1,0:T(8,128)(2,1)S(1)} %get-tuple-element.24), channel_id=1, source_target_pairs={{0,8},{4,12},{8,16},{12,20},{16,24},{20,28},{24,32},{28,36},{32,40... | collective-permute-start | bytes 2359304 | tf_op jit(solution)/shard_map/ppermute | solution.py:19
  79.2 4.1 %collective-permute-start.7 = (bf16[512,768]{1,0:T(8,128)(2,1)S(1)}, bf16[512,768]{1,0:T(8,128)(2,1)S(1)}, u32[]{:S(2)}, u32[]{:S(2)}) collective-permute-start(bf16[512,768]{1,0:T(8,128)(2,1)S(1)} %get-tuple-element.25), channel_id=1, source_target_pairs={{8,0},{12,4},{16,8},{20,12},{24,16},{28,20},{32,24},{36,28},{40,32... | collective-permute-start | bytes 2359304 | tf_op jit(solution)/shard_map/ppermute | solution.py:19
  83.4 15.8 %collective-permute-done.6 = bf16[512,768]{1,0:T(8,128)(2,1)S(1)} collective-permute-done((bf16[512,768]{1,0:T(8,128)(2,1)S(1)}, bf16[512,768]{1,0:T(8,128)(2,1)S(1)}, u32[]{:S(2)}, u32[]{:S(2)}) %collective-permute-start.6) | collective-permute-done | bytes 786464 | tf_op jit(solution)/shard_map/ppermute | solution.py:19
  99.1 5.2 %collective-permute-done.7 = bf16[512,768]{1,0:T(8,128)(2,1)S(1)} collective-permute-done((bf16[512,768]{1,0:T(8,128)(2,1)S(1)}, bf16[512,768]{1,0:T(8,128)(2,1)S(1)}, u32[]{:S(2)}, u32[]{:S(2)}) %collective-permute-start.7) | collective-permute-done | bytes 786464 | tf_op jit(solution)/shard_map/ppermute | solution.py:19
  104.9 1.1 fusion.5
  106.0 1.0 copy.31
  107.0 0.9 copy.27
  107.9 1.0 copy.32
  108.9 0.9 copy.28
  109.9 1.9 %copy.30 = bf16[512,384]{1,0:T(8,128)(2,1)} copy(bf16[512,384]{0,1:T(8,128)(2,1)} %bitcast.27) | data formatting | bytes 786432
  (33 shorter events, 1.1 us)
Async XLA Ops:
  7.2 37.2 %copy-start = (bf16[384,1536]{1,0:T(8,128)(2,1)S(1)}, bf16[384,1536]{1,0:T(8,128)(2,1)}, u32[]{:S(2)}) copy-start(bf16[384,1536]{1,0:T(8,128)(2,1)} %param.10) | copy-start | bytes 3538948
  7.2 37.2 %all-gather.2.cloned.1.call-start = ((), (), s32[]{:S(2)}) async-start(), calls=%async_computation.1 | async-start | bytes 1966080 | tf_op jit(solution)/shard_map/all_gather | solution.py:135
  7.9 102.0 %reduce-scatter.4.cloned.1.call-start = ((), (), s32[]{:S(2)}) async-start(), calls=%async_computation.2 | async-start | bytes 1966080
  11.9 31.4 %copy-start.7 = (s32[512]{0:T(512)S(1)}, s32[512]{0:T(512)}, u32[]{:S(2)}) copy-start(s32[512]{0:T(512)} %param.13) | copy-start | bytes 6148
  11.9 32.3 %copy-start.9 = (s32[64,2]{0,1:T(2,128)S(1)}, s32[64,2]{0,1:T(2,128)}, u32[]{:S(2)}) copy-start(s32[64,2]{0,1:T(2,128)} %param.12) | copy-start | bytes 1540
  11.9 21.7 %collective-permute-start = (bf16[512,768]{1,0:T(8,128)(2,1)S(1)}, bf16[512,768]{1,0:T(8,128)(2,1)S(1)}, u32[]{:S(2)}, u32[]{:S(2)}) collective-permute-start(bf16[512,768]{1,0:T(8,128)(2,1)S(1)} %reshape.83.kv0_ref), channel_id=1, source_target_pairs={{0,8},{4,12},{8,16},{12,20},{16,24},{20,28},{24,32},{28,36},{32,40... | collective-permute-start | bytes 2359304 | tf_op jit(solution)/shard_map/ppermute | solution.py:19
  16.9 24.3 %collective-permute-start.2 = (bf16[512,768]{1,0:T(8,128)(2,1)S(1)}, bf16[512,768]{1,0:T(8,128)(2,1)}, u32[]{:S(2)}, u32[]{:S(2)}) collective-permute-start(bf16[512,768]{1,0:T(8,128)(2,1)S(1)} %reshape.83.kv0_ref), channel_id=1, source_target_pairs={{8,0},{12,4},{16,8},{20,12},{24,16},{28,20},{32,24},{36,28},{40,32... | collective-permute-start | bytes 2359304 | tf_op jit(solution)/shard_map/ppermute | solution.py:19
  18.8 28.1 %collective-permute-start.1 = (bf16[512,768]{1,0:T(8,128)(2,1)S(1)}, bf16[512,768]{1,0:T(8,128)(2,1)S(1)}, u32[]{:S(2)}, u32[]{:S(2)}) collective-permute-start(bf16[512,768]{1,0:T(8,128)(2,1)S(1)} %reshape.83.kv0_ref), channel_id=1, source_target_pairs={{0,4},{4,0},{8,12},{12,8},{16,20},{20,16},{24,28},{28,24},{32,36},... | collective-permute-start | bytes 2359304 | tf_op jit(solution)/shard_map/ppermute | solution.py:24
  43.3 4.5 %collective-permute-start.3 = (bf16[512,768]{1,0:T(8,128)(2,1)}, bf16[512,768]{1,0:T(8,128)(2,1)}, u32[]{:S(2)}, u32[]{:S(2)}) collective-permute-start(bf16[512,768]{1,0:T(8,128)(2,1)} %broadcast_select_fusion.2), channel_id=1, source_target_pairs={{0,4},{4,0},{8,12},{12,8},{16,20},{20,16},{24,28},{28,24},{32,36},... | collective-permute-start | bytes 2359304 | tf_op jit(solution)/shard_map/ppermute | solution.py:24
  44.4 3.4 %copy-start.3 = (s32[512,1]{1,0:T(8,128)S(1)}, s32[512,1]{1,0:T(8,128)}, u32[]{:S(2)}) copy-start(s32[512,1]{1,0:T(8,128)} %copy.24.srow_ref) | copy-start | bytes 6148
  44.4 3.4 %copy-start.6 = (bf16[512,384]{1,0:T(8,128)(2,1)S(1)}, bf16[512,384]{1,0:T(8,128)(2,1)}, u32[]{:S(2)}) copy-start(bf16[512,384]{1,0:T(8,128)(2,1)} %q_ref.1) | copy-start | bytes 1179652
  46.9 0.9 copy-start.4
  47.8 1.1 copy-start.5
  64.5 0.9 copy-start.1
  68.0 3.1 %copy-start.2 = (bf16[512,768]{1,0:T(8,128)(2,1)S(1)}, bf16[512,768]{1,0:T(8,128)(2,1)}, u32[]{:S(2)}) copy-start(bf16[512,768]{1,0:T(8,128)(2,1)} %copy-done.1) | copy-start | bytes 2359300
  72.2 3.2 %collective-permute-start.5 = (bf16[512,768]{1,0:T(8,128)(2,1)}, bf16[512,768]{1,0:T(8,128)(2,1)}, u32[]{:S(2)}, u32[]{:S(2)}) collective-permute-start(bf16[512,768]{1,0:T(8,128)(2,1)} %get-tuple-element.27), channel_id=1, source_target_pairs={{0,4},{4,0},{8,12},{12,8},{16,20},{20,16},{24,28},{28,24},{32,36},... | collective-permute-start | bytes 2359304 | tf_op jit(solution)/shard_map/ppermute | solution.py:24
  75.3 8.1 %collective-permute-start.4 = (bf16[512,768]{1,0:T(8,128)(2,1)S(1)}, bf16[512,768]{1,0:T(8,128)(2,1)S(1)}, u32[]{:S(2)}, u32[]{:S(2)}) collective-permute-start(bf16[512,768]{1,0:T(8,128)(2,1)S(1)} %get-tuple-element.26), channel_id=1, source_target_pairs={{0,4},{4,0},{8,12},{12,8},{16,20},{20,16},{24,28},{28,24},{32,36},... | collective-permute-start | bytes 2359304 | tf_op jit(solution)/shard_map/ppermute | solution.py:24
  75.4 29.0 %copy-start.8 = (f32[512,768]{1,0:T(8,128)S(1)}, f32[512,768]{1,0:T(8,128)}, u32[]{:S(2)}) copy-start(f32[512,768]{1,0:T(8,128)} %get-tuple-element.11) | copy-start | bytes 4718596
  77.3 21.8 %collective-permute-start.6 = (bf16[512,768]{1,0:T(8,128)(2,1)S(1)}, bf16[512,768]{1,0:T(8,128)(2,1)S(1)}, u32[]{:S(2)}, u32[]{:S(2)}) collective-permute-start(bf16[512,768]{1,0:T(8,128)(2,1)S(1)} %get-tuple-element.24), channel_id=1, source_target_pairs={{0,8},{4,12},{8,16},{12,20},{16,24},{20,28},{24,32},{28,36},{32,40... | collective-permute-start | bytes 2359304 | tf_op jit(solution)/shard_map/ppermute | solution.py:19
  79.2 25.1 %collective-permute-start.7 = (bf16[512,768]{1,0:T(8,128)(2,1)S(1)}, bf16[512,768]{1,0:T(8,128)(2,1)S(1)}, u32[]{:S(2)}, u32[]{:S(2)}) collective-permute-start(bf16[512,768]{1,0:T(8,128)(2,1)S(1)} %get-tuple-element.25), channel_id=1, source_target_pairs={{8,0},{12,4},{16,8},{20,12},{24,16},{28,20},{32,24},{36,28},{40,32... | collective-permute-start | bytes 2359304 | tf_op jit(solution)/shard_map/ppermute | solution.py:19
Sparse Core Ops, SparseCore 0:
  9.8 29.6 all-gather.1
  68.1 25.8 reduce-scatter.3

commit v2 on v1

--- a/solution.py
+++ b/solution.py
@@ -17,6 +17,56 @@
     devices = range(lax.axis_size(axis))
     route = [(i - distance, i) for i in devices if i - distance in devices]
     return lax.ppermute(block, axis, route)
+
+
+def ring_shift(block, axis, distance):
+    size = lax.axis_size(axis)
+    return lax.ppermute(block, axis, [(i, (i + distance) % size) for i in range(size)])
+
+
+def head_slice(array, group, width):
+    return lax.dynamic_slice_in_dim(array, group * width, width, 1)
+
+
+def fold_cotangent(cotangent, out_weight):
+    groups = lax.axis_size("head")
+    me = lax.axis_index("head")
+    rows, width = cotangent.shape
+    half = rows // 2
+    from_prev = ring_shift(cotangent, "head", 1)
+    from_next = ring_shift(cotangent, "head", -1)
+    far_a = ring_shift(from_prev[:half], "head", 1)
+    far_b = ring_shift(from_next[half:], "head", -1)
+    far = jnp.concatenate([far_a, far_b], axis=0)
+    nt = (((1,), (1,)), ((), ()))
+    acc = None
+    for piece, group in ((cotangent, me), (from_prev, me - 1), (from_next, me + 1), (far, me + 2)):
+        w_cols = head_slice(out_weight, group % groups, width)
+        part = lax.dot_general(piece, w_cols, nt, preferred_element_type=jnp.float32)
+        acc = part if acc is None else acc + part
+    return acc.astype(jnp.bfloat16)
+
+
+def project_out(attn, out_weight):
+    groups = lax.axis_size("head")
+    me = lax.axis_index("head")
+    rows, width = attn.shape
+    half = rows // 2
+
+    def part(group):
+        w_cols = head_slice(out_weight, group % groups, width)
+        return jnp.dot(attn, w_cols, preferred_element_type=jnp.float32)
+
+    far = part(me + 2).astype(jnp.bfloat16)
+    got_a = ring_shift(far[:half], "head", 1)
+    got_b = ring_shift(far[half:], "head", -1)
+    zeros = jnp.zeros((half, width), jnp.float32)
+    up = part(me + 1) + jnp.concatenate([got_a.astype(jnp.float32), zeros], axis=0)
+    down = part(me - 1) + jnp.concatenate([zeros, got_b.astype(jnp.float32)], axis=0)
+    from_prev = ring_shift(up.astype(jnp.bfloat16), "head", 1)
+    from_next = ring_shift(down.astype(jnp.bfloat16), "head", -1)
+    total = part(me) + from_prev.astype(jnp.float32) + from_next.astype(jnp.float32)
+    return total.astype(jnp.bfloat16)
 
 
 def partner_swap(block, axis):
@@ -132,10 +182,7 @@
     seq_index = lax.axis_index("seq")
     tok_rows, columns = queries.shape
     parity = seq_index % 2
-    cot_full = lax.all_gather(cotangent, "head", axis=1, tiled=True)
-    grad_attn = lax.dot_general(
-        cot_full, out_weight, (((1,), (1,)), ((), ())), preferred_element_type=jnp.float32
-    ).astype(jnp.bfloat16)
+    grad_attn = fold_cotangent(cotangent, out_weight)
     own_kv = pack_heads(keys, values)
     from_left2 = shifted(own_kv, "seq", 2)
     from_right2 = shifted(own_kv, "seq", -2)
@@ -148,8 +195,7 @@
     sel = sel.astype(jnp.int32)
     cands = (from_left2, partner_own, partner_relay, from_right2)
     attn, grad_q, self_term, term1, term2 = attention(sel, queries, own_kv, cands, grad_attn, shot_ids)
-    partial_out = jnp.dot(attn, out_weight, preferred_element_type=jnp.float32)
-    attn_out = lax.psum_scatter(partial_out.astype(jnp.bfloat16), "head", scatter_dimension=1, tiled=True)
+    attn_out = project_out(attn, out_weight)
     zero = jnp.zeros_like(term1)
 
     def term_for(offset):

time: 119 us -> 113 us (0.950)
  between operations: 19.5 us -> 6.14 us
  starting transfers between devices: 13.7 us -> 21.5 us
  local copies, waits for them, and re-layouts: 16.7 us -> 11.7 us
  matrix products: 3.43 us -> 8.12 us
    ppermute x4, waiting for transfers between devices: 43.3 us -> 25.1 us  [shifted(): return lax.ppermute(block, axis, route)]
    ppermute x0 -> x8, waiting for transfers between devices: none -> 18.1 us  [ring_shift(): lax.ppermute(block, axis, [(i, (i + distance) % size) for i in range(size)])]
    ppermute x0 -> x8, starting transfers between devices: none -> 8.49 us  [ring_shift(): lax.ppermute(block, axis, [(i, (i + distance) % size) for i in range(size)])]
    unnamed x28 -> x24, local copies, waits for them, and re-layouts: 12.6 us -> 6.55 us
    dot_general x2 -> x8, matrix products: 3.43 us -> 8.12 us  [the longest x4 5.76 us: fold_cotangent(): lax.dot_general(piece, w_cols, nt, preferred_element_type=jnp.float32)]
    slice x0 -> x3, local copies, waits for them, and re-layouts: none -> 1.69 us  [the longest x1 0.95 us: fold_cotangent(): far_b = ring_shift(from_next[half:], 'head', -1)]
  transfers between devices with their start and end apart: 10 -> 16, of which waited for: 4 -> 9; matrix products, arithmetic and copies ran while one was open for 16% -> 13% of each run, Pallas kernels for 0% -> 0%
where the time goes in v2:
time: 113 us; the launch traced here: 112 us
  waiting for transfers between devices  43.2 us (38%)
  starting transfers between devices  21.5 us (19%)
  Pallas kernels  15.6 us (14%)
  local copies, waits for them, and re-layouts  11.7 us (10%)
  matrix products  8.12 us (7%)
  between operations  6.14 us (5%)
  other arithmetic  5.96 us (5%)
    ppermute x4, waiting for transfers between devices, shifted(): return lax.ppermute(block, axis, route)  25.1 us
    ppermute x8, waiting for transfers between devices, ring_shift(): lax.ppermute(block, axis, [(i, (i + distance) % size) for i in range(size)])  18.1 us
    pallas_call x1, Pallas kernels, attention(): pl.pallas_call(attn_kernel, grid_spec=grid_spec, out_shape=out_shape, com...  15.6 us
    ppermute x4, starting transfers between devices, shifted(): return lax.ppermute(block, axis, route)  12.7 us
    ppermute x8, starting transfers between devices, ring_shift(): lax.ppermute(block, axis, [(i, (i + distance) % size) for i in range(size)])  8.49 us
    unnamed x24, local copies, waits for them, and re-layouts  6.55 us
    dot_general x4, matrix products, fold_cotangent(): lax.dot_general(piece, w_cols, nt, preferred_element_type=jnp.float32)  5.76 us
    dot_general x4, matrix products, part(): return jnp.dot(attn, w_cols, preferred_element_type=jnp.float32)  2.36 us
  transfers between devices with their start and end apart: 16, of which 9 were waited for; matrix products, arithmetic and copies ran while one was open for 13% of the time, Pallas kernels for 0%

profile of v2, /device:TPU:126, one launch (start us, length us, event | category | flops | bytes accessed | tf_op | source)
XLA Modules:
  0.0 112.2 jit_solution(15039410359248019809)
XLA Ops:
  0.6 1.3 %copy.16 = bf16[512,384]{0,1:T(8,128)(2,1)S(1)} copy(bf16[512,384]{1,0:T(8,128)(2,1)} %param.8) | data formatting | bytes 786432 | tf_op args[1]
  1.9 1.2 %copy.17 = bf16[512,384]{0,1:T(8,128)(2,1)S(1)} copy(bf16[512,384]{1,0:T(8,128)(2,1)} %param.9) | data formatting | bytes 786432 | tf_op args[2]
  3.2 1.1 %copy.18 = bf16[512,3,2,128]{3,2,1,0:T(2,128)(2,1)S(1)} copy(bf16[512,3,2,128]{0,3,1,2:T(8,128)(2,1)S(1)} %pad_maximum_fusion) | data formatting | bytes 1572864 | tf_op jit(solution)/shard_map/concatenate | solution.py:82
  4.7 5.0 %collective-permute-start = (bf16[512,768]{1,0:T(8,128)(2,1)S(1)}, bf16[512,768]{1,0:T(8,128)(2,1)S(1)}, u32[]{:S(2)}, u32[]{:S(2)}) collective-permute-start(bf16[512,768]{1,0:T(8,128)(2,1)S(1)} %reshape.83.kv0_ref), channel_id=1, source_target_pairs={{0,8},{4,12},{8,16},{12,20},{16,24},{20,28},{24,32},{28,36},{32,40... | collective-permute-start | bytes 2359304 | tf_op jit(solution)/shard_map/ppermute | solution.py:19
  9.6 1.9 %collective-permute-start.2 = (bf16[512,768]{1,0:T(8,128)(2,1)S(1)}, bf16[512,768]{1,0:T(8,128)(2,1)}, u32[]{:S(2)}, u32[]{:S(2)}) collective-permute-start(bf16[512,768]{1,0:T(8,128)(2,1)S(1)} %reshape.83.kv0_ref), channel_id=1, source_target_pairs={{8,0},{12,4},{16,8},{20,12},{24,16},{28,20},{32,24},{36,28},{40,32... | collective-permute-start | bytes 2359304 | tf_op jit(solution)/shard_map/ppermute | solution.py:19
  11.9 1.8 %collective-permute-start.5 = (bf16[512,384]{1,0:T(8,128)(2,1)}, bf16[512,384]{1,0:T(8,128)(2,1)}, u32[]{:S(2)}, u32[]{:S(2)}) collective-permute-start(bf16[512,384]{1,0:T(8,128)(2,1)} %param.11), channel_id=1, source_target_pairs={{0,3},{1,0},{2,1},{3,2},{4,7},{5,4},{6,5},{7,6},{8,11},{9,8},{10,9... | collective-permute-start | bytes 1179656 | tf_op jit(solution)/shard_map/ppermute | solution.py:24
  13.9 2.4 %fusion.22 = f32[384,512]{0,1:T(8,128)} fusion(bf16[512,384]{1,0:T(8,128)(2,1)} %param.11, bf16[384,1536]{1,0:T(8,128)(2,1)S(1)} %copy-done, s32[]{:T(128)S(6)} %select_n.150), kind=kOutput, calls=%fused_computation.37 | convolution fusion | flops 150994944 | bytes 1474564 | tf_op jit(solution)/shard_map/dot_general | solution.py:45
  16.2 10.2 %collective-permute-done.c0_ref = bf16[512,768]{1,0:T(8,128)(2,1)S(1)} collective-permute-done((bf16[512,768]{1,0:T(8,128)(2,1)S(1)}, bf16[512,768]{1,0:T(8,128)(2,1)S(1)}, u32[]{:S(2)}, u32[]{:S(2)}) %collective-permute-start) | collective-permute-done | bytes 786464 | tf_op jit(solution)/shard_map/ppermute | solution.py:19
  26.4 7.5 %collective-permute-done.2.c3_ref = bf16[512,768]{1,0:T(8,128)(2,1)} collective-permute-done((bf16[512,768]{1,0:T(8,128)(2,1)S(1)}, bf16[512,768]{1,0:T(8,128)(2,1)}, u32[]{:S(2)}, u32[]{:S(2)}) %collective-permute-start.2) | collective-permute-done | bytes 786464 | tf_op jit(solution)/shard_map/ppermute | solution.py:19
  34.0 2.1 %broadcast_select_fusion.2 = bf16[512,768]{1,0:T(8,128)(2,1)} fusion(bf16[512,768]{1,0:T(8,128)(2,1)} %collective-permute-done.2.c3_ref, bf16[512,768]{1,0:T(8,128)(2,1)S(1)} %collective-permute-done.c0_ref, pred[]{:T(512)S(6)} %eq.97), kind=kLoop, calls=%fused_computation.25 | loop fusion | flops 393216 | bytes 2359297 | tf_op jit(solution)/shard_map/jit(_where)/select_n | solution.py:190
  39.7 0.9 slice.41
  40.7 1.9 %collective-permute-start.7 = (bf16[256,384]{1,0:T(8,128)(2,1)S(1)}, bf16[256,384]{1,0:T(8,128)(2,1)S(1)}, u32[]{:S(2)}, u32[]{:S(2)}) collective-permute-start(bf16[256,384]{1,0:T(8,128)(2,1)S(1)} %slice.41), channel_id=1, source_target_pairs={{0,3},{1,0},{2,1},{3,2},{4,7},{5,4},{6,5},{7,6},{8,11},{9,8},{10,9... | collective-permute-start | bytes 589832 | tf_op jit(solution)/shard_map/ppermute | solution.py:24
  42.5 1.5 %convolution_add_fusion.4 = f32[384,512]{0,1:T(8,128)S(1)} fusion(f32[384,512]{0,1:T(8,128)} %fusion.22, bf16[512,384]{1,0:T(8,128)(2,1)S(1)} %collective-permute-done.4, bf16[384,1536]{1,0:T(8,128)(2,1)S(1)} %copy-done, s32[]{:T(128)S(6)} %select_n.152), kind=kOutput, calls=%fused_computation.12 | convolution fusion | flops 151191552 | bytes 2260996 | tf_op jit(solution)/shard_map/dot_general | solution.py:45
  44.1 2.7 %collective-permute-done.6 = bf16[256,384]{1,0:T(8,128)(2,1)S(1)} collective-permute-done((bf16[256,384]{1,0:T(8,128)(2,1)S(1)}, bf16[256,384]{1,0:T(8,128)(2,1)S(1)}, u32[]{:S(2)}, u32[]{:S(2)}) %collective-permute-start.6) | collective-permute-done | bytes 196640 | tf_op jit(solution)/shard_map/ppermute | solution.py:24
  46.8 2.3 %collective-permute-done.7 = bf16[256,384]{1,0:T(8,128)(2,1)S(1)} collective-permute-done((bf16[256,384]{1,0:T(8,128)(2,1)S(1)}, bf16[256,384]{1,0:T(8,128)(2,1)S(1)}, u32[]{:S(2)}, u32[]{:S(2)}) %collective-permute-start.7) | collective-permute-done | bytes 196640 | tf_op jit(solution)/shard_map/ppermute | solution.py:24
  49.5 1.5 %fusion.8.g_ref = bf16[512,384]{1,0:T(8,128)(2,1)S(1)} fusion(f32[512,384]{1,0:T(8,128)S(1)} %fusion.11, f32[384,512]{0,1:T(8,128)S(1)} %convolution_add_fusion.4, bf16[512,384]{1,0:T(8,128)(2,1)} %collective-permute-done.5, bf16[384,1536]{1,0:T(8,128)(2,1)S(1)} %copy-done, s32[]{:T(128)S(6)} %select_n.154), kind=kOutput, calls=%fused_computation.16 | convolution fusion | flops 151584768 | bytes 2654212 | tf_op jit(solution)/shard_map/dot_general | solution.py:45
  51.0 15.6 %shard_map.102 = (bf16[512,384]{1,0:T(8,128)(2,1)S(1)}, bf16[512,384]{1,0:T(8,128)(2,1)}, f32[512,768]{1,0:T(8,128)}, bf16[512,768]{1,0:T(8,128)(2,1)S(1)}, bf16[512,768]{1,0:T(8,128)(2,1)S(1)}) custom-call(s32[2]{0:T(128)S(1)} %get-tuple-element.18.sel_ref, bf16[512,384]{1,0:T(8,128)(2,1)S(1)} %copy-done.5, bf16[512,768]{1,0:T(8,128)(2,1)S(1)} %reshape.83.kv0_ref, ...), custom_call_target="tpu_custom_call" | custom-call | tf_op jit(solution)/shard_map/pallas_call | solution.py:172
  66.6 1.4 %broadcast_select_fusion.1 = (bf16[512,768]{1,0:T(8,128)(2,1)}, bf16[512,768]{1,0:T(8,128)(2,1)}) fusion(pred[]{:T(512)S(6)} %eq.97, bf16[512,768]{1,0:T(8,128)(2,1)S(1)} %get-tuple-element.12, bf16[512,768]{1,0:T(8,128)(2,1)S(1)} %get-tuple-element.13, pred[]{:T(512)} %bitcast.6, pred[]{:T(512)} %bitcast.5, pred[]{:T(512)} %bitcast.8, pred[]{:T(512)} %bitcast.7), kind=kLoop, calls=%fused_computation.24 | loop fusion | flops 2359296 | bytes 3145733 | tf_op jit(solution)/shard_map/jit(_where)/select_n | solution.py:206
  72.7 1.7 %collective-permute-start.10 = (bf16[256,384]{1,0:T(8,128)(2,1)S(1)}, bf16[256,384]{1,0:T(8,128)(2,1)S(1)}, u32[]{:S(2)}, u32[]{:S(2)}) collective-permute-start(bf16[256,384]{1,0:T(8,128)(2,1)S(1)} %get-tuple-element.27), channel_id=1, source_target_pairs={{0,3},{1,0},{2,1},{3,2},{4,7},{5,4},{6,5},{7,6},{8,11},{9,8},{10,9... | collective-permute-start | bytes 589832 | tf_op jit(solution)/shard_map/ppermute | solution.py:24
  74.4 2.6 %collective-permute-done.8 = bf16[256,384]{1,0:T(8,128)(2,1)S(1)} collective-permute-done((bf16[256,384]{1,0:T(8,128)(2,1)}, bf16[256,384]{1,0:T(8,128)(2,1)S(1)}, u32[]{:S(2)}, u32[]{:S(2)}) %collective-permute-start.8) | collective-permute-done | bytes 196640 | tf_op jit(solution)/shard_map/ppermute | solution.py:24
  77.4 1.6 %collective-permute-start.9 = (bf16[512,384]{1,0:T(8,128)(2,1)S(1)}, bf16[512,384]{1,0:T(8,128)(2,1)S(1)}, u32[]{:S(2)}, u32[]{:S(2)}) collective-permute-start(bf16[512,384]{1,0:T(8,128)(2,1)S(1)} %fusion.9), channel_id=1, source_target_pairs={{0,1},{1,2},{2,3},{3,0},{4,5},{5,6},{6,7},{7,4},{8,9},{9,10},{10,1... | collective-permute-start | bytes 1179656 | tf_op jit(solution)/shard_map/ppermute | solution.py:24
  79.0 1.8 %fusion.1 = (bf16[512,768]{1,0:T(8,128)(2,1)S(1)}, bf16[512,768]{1,0:T(8,128)(2,1)S(1)}) fusion(bf16[512,768]{1,0:T(8,128)(2,1)} %collective-permute-done.13, bf16[512,768]{1,0:T(8,128)(2,1)S(1)} %copy-done.2, bf16[512,768]{1,0:T(8,128)(2,1)S(1)} %copy-done.4, pred[]{:T(512)} %bitcast.10, pred[]{:T(512)} %bitcast.9, pred[]{:T(512)S(6)} %eq.97, pred[]{:T(512)S(6)} %eq.114, ...), kind=kLoop, calls=%fused_computation.3 | loop fusion | flops 5111808 | bytes 3932166 | tf_op jit(solution)/shard_map/convert_element_type | solution.py:212
  80.7 1.9 %collective-permute-start.14 = (bf16[512,768]{1,0:T(8,128)(2,1)S(1)}, bf16[512,768]{1,0:T(8,128)(2,1)S(1)}, u32[]{:S(2)}, u32[]{:S(2)}) collective-permute-start(bf16[512,768]{1,0:T(8,128)(2,1)S(1)} %get-tuple-element.20), channel_id=1, source_target_pairs={{0,8},{4,12},{8,16},{12,20},{16,24},{20,28},{24,32},{28,36},{32,40... | collective-permute-start | bytes 2359304 | tf_op jit(solution)/shard_map/ppermute | solution.py:19
  82.7 3.9 %collective-permute-start.15 = (bf16[512,768]{1,0:T(8,128)(2,1)S(1)}, bf16[512,768]{1,0:T(8,128)(2,1)S(1)}, u32[]{:S(2)}, u32[]{:S(2)}) collective-permute-start(bf16[512,768]{1,0:T(8,128)(2,1)S(1)} %get-tuple-element.21), channel_id=1, source_target_pairs={{8,0},{12,4},{16,8},{20,12},{24,16},{28,20},{32,24},{36,28},{40,32... | collective-permute-start | bytes 2359304 | tf_op jit(solution)/shard_map/ppermute | solution.py:19
  88.1 10.0 %collective-permute-done.11 = bf16[512,384]{1,0:T(8,128)(2,1)S(1)} collective-permute-done((bf16[512,384]{1,0:T(8,128)(2,1)S(1)}, bf16[512,384]{1,0:T(8,128)(2,1)S(1)}, u32[]{:S(2)}, u32[]{:S(2)}) %collective-permute-start.11) | collective-permute-done | bytes 393248 | tf_op jit(solution)/shard_map/ppermute | solution.py:24
  98.1 1.2 %fusion.7 = bf16[512,384]{1,0:T(8,128)(2,1)} fusion(bf16[512,384]{1,0:T(8,128)(2,1)S(1)} %get-tuple-element.9, bf16[512,384]{1,0:T(8,128)(2,1)S(1)} %collective-permute-done.11, bf16[512,384]{1,0:T(8,128)(2,1)S(1)} %collective-permute-done.9, bf16[384,1536]{1,0:T(8,128)(2,1)S(1)} %copy-done, s32[]{:T(128)S(6)} %select_n.150), kind=kOutput, calls=%fused_computation.15 | convolution fusion | flops 151977984 | bytes 1867780 | tf_op jit(solution)/shard_map/dot_general | solution.py:58
  99.3 2.1 %collective-permute-done.14 = bf16[512,768]{1,0:T(8,128)(2,1)S(1)} collective-permute-done((bf16[512,768]{1,0:T(8,128)(2,1)S(1)}, bf16[512,768]{1,0:T(8,128)(2,1)S(1)}, u32[]{:S(2)}, u32[]{:S(2)}) %collective-permute-start.14) | collective-permute-done | bytes 786464 | tf_op jit(solution)/shard_map/ppermute | solution.py:19
  101.5 5.2 %collective-permute-done.15 = bf16[512,768]{1,0:T(8,128)(2,1)S(1)} collective-permute-done((bf16[512,768]{1,0:T(8,128)(2,1)S(1)}, bf16[512,768]{1,0:T(8,128)(2,1)S(1)}, u32[]{:S(2)}, u32[]{:S(2)}) %collective-permute-start.15) | collective-permute-done | bytes 786464 | tf_op jit(solution)/shard_map/ppermute | solution.py:19
  107.3 1.1 fusion.36
  108.4 1.0 copy.30
  110.3 1.0 copy.31
  111.3 0.9 copy.26
  (48 shorter events, 7.7 us)
Async XLA Ops:
  0.6 13.2 %copy-start = (bf16[384,1536]{1,0:T(8,128)(2,1)S(1)}, bf16[384,1536]{1,0:T(8,128)(2,1)}, u32[]{:S(2)}) copy-start(bf16[384,1536]{1,0:T(8,128)(2,1)} %param.10) | copy-start | bytes 3538948
  4.3 9.4 %copy-start.8 = (s32[64,2]{0,1:T(2,128)S(1)}, s32[64,2]{0,1:T(2,128)}, u32[]{:S(2)}) copy-start(s32[64,2]{0,1:T(2,128)} %param.12) | copy-start | bytes 1540
  4.7 21.7 %collective-permute-start = (bf16[512,768]{1,0:T(8,128)(2,1)S(1)}, bf16[512,768]{1,0:T(8,128)(2,1)S(1)}, u32[]{:S(2)}, u32[]{:S(2)}) collective-permute-start(bf16[512,768]{1,0:T(8,128)(2,1)S(1)} %reshape.83.kv0_ref), channel_id=1, source_target_pairs={{0,8},{4,12},{8,16},{12,20},{16,24},{20,28},{24,32},{28,36},{32,40... | collective-permute-start | bytes 2359304 | tf_op jit(solution)/shard_map/ppermute | solution.py:19
  9.6 24.3 %collective-permute-start.2 = (bf16[512,768]{1,0:T(8,128)(2,1)S(1)}, bf16[512,768]{1,0:T(8,128)(2,1)}, u32[]{:S(2)}, u32[]{:S(2)}) collective-permute-start(bf16[512,768]{1,0:T(8,128)(2,1)S(1)} %reshape.83.kv0_ref), channel_id=1, source_target_pairs={{8,0},{12,4},{16,8},{20,12},{24,16},{28,20},{32,24},{36,28},{40,32... | collective-permute-start | bytes 2359304 | tf_op jit(solution)/shard_map/ppermute | solution.py:19
  11.6 27.8 %collective-permute-start.4 = (bf16[512,384]{1,0:T(8,128)(2,1)}, bf16[512,384]{1,0:T(8,128)(2,1)S(1)}, u32[]{:S(2)}, u32[]{:S(2)}) collective-permute-start(bf16[512,384]{1,0:T(8,128)(2,1)} %param.11), channel_id=1, source_target_pairs={{0,1},{1,2},{2,3},{3,0},{4,5},{5,6},{6,7},{7,4},{8,9},{9,10},{10,1... | collective-permute-start | bytes 1179656 | tf_op jit(solution)/shard_map/ppermute | solution.py:24
  11.9 27.8 %collective-permute-start.5 = (bf16[512,384]{1,0:T(8,128)(2,1)}, bf16[512,384]{1,0:T(8,128)(2,1)}, u32[]{:S(2)}, u32[]{:S(2)}) collective-permute-start(bf16[512,384]{1,0:T(8,128)(2,1)} %param.11), channel_id=1, source_target_pairs={{0,3},{1,0},{2,1},{3,2},{4,7},{5,4},{6,5},{7,6},{8,11},{9,8},{10,9... | collective-permute-start | bytes 1179656 | tf_op jit(solution)/shard_map/ppermute | solution.py:24
  13.7 37.3 %collective-permute-start.1 = (bf16[512,768]{1,0:T(8,128)(2,1)S(1)}, bf16[512,768]{1,0:T(8,128)(2,1)}, u32[]{:S(2)}, u32[]{:S(2)}) collective-permute-start(bf16[512,768]{1,0:T(8,128)(2,1)S(1)} %reshape.83.kv0_ref), channel_id=1, source_target_pairs={{0,4},{4,0},{8,12},{12,8},{16,20},{20,16},{24,28},{28,24},{32,36},... | collective-permute-start | bytes 2359304 | tf_op jit(solution)/shard_map/ppermute | solution.py:74
  16.2 23.0 %copy-start.6 = (s32[512]{0:T(512)S(1)}, s32[512]{0:T(512)}, u32[]{:S(2)}) copy-start(s32[512]{0:T(512)} %param.13) | copy-start | bytes 6148
  36.1 14.9 %collective-permute-start.3 = (bf16[512,768]{1,0:T(8,128)(2,1)}, bf16[512,768]{1,0:T(8,128)(2,1)}, u32[]{:S(2)}, u32[]{:S(2)}) collective-permute-start(bf16[512,768]{1,0:T(8,128)(2,1)} %broadcast_select_fusion.2), channel_id=1, source_target_pairs={{0,4},{4,0},{8,12},{12,8},{16,20},{20,16},{24,28},{28,24},{32,36},... | collective-permute-start | bytes 2359304 | tf_op jit(solution)/shard_map/ppermute | solution.py:74
  39.4 7.4 %collective-permute-start.6 = (bf16[256,384]{1,0:T(8,128)(2,1)S(1)}, bf16[256,384]{1,0:T(8,128)(2,1)S(1)}, u32[]{:S(2)}, u32[]{:S(2)}) collective-permute-start(bf16[256,384]{1,0:T(8,128)(2,1)S(1)} %slice.40), channel_id=1, source_target_pairs={{0,1},{1,2},{2,3},{3,0},{4,5},{5,6},{6,7},{7,4},{8,9},{9,10},{10,1... | collective-permute-start | bytes 589832 | tf_op jit(solution)/shard_map/ppermute | solution.py:24
  40.7 8.4 %collective-permute-start.7 = (bf16[256,384]{1,0:T(8,128)(2,1)S(1)}, bf16[256,384]{1,0:T(8,128)(2,1)S(1)}, u32[]{:S(2)}, u32[]{:S(2)}) collective-permute-start(bf16[256,384]{1,0:T(8,128)(2,1)S(1)} %slice.41), channel_id=1, source_target_pairs={{0,3},{1,0},{2,1},{3,2},{4,7},{5,4},{6,5},{7,6},{8,11},{9,8},{10,9... | collective-permute-start | bytes 589832 | tf_op jit(solution)/shard_map/ppermute | solution.py:24
  49.5 1.5 %copy-start.5 = (bf16[512,384]{1,0:T(8,128)(2,1)S(1)}, bf16[512,384]{1,0:T(8,128)(2,1)}, u32[]{:S(2)}) copy-start(bf16[512,384]{1,0:T(8,128)(2,1)} %q_ref.1) | copy-start | bytes 1179652
  66.6 1.4 %copy-start.1 = (bf16[512,768]{1,0:T(8,128)(2,1)}, bf16[512,768]{1,0:T(8,128)(2,1)S(1)}, u32[]{:S(2)}) copy-start(bf16[512,768]{1,0:T(8,128)(2,1)S(1)} %get-tuple-element.12) | copy-start | bytes 2359300
  66.6 1.7 %copy-start.3 = (bf16[512,768]{1,0:T(8,128)(2,1)}, bf16[512,768]{1,0:T(8,128)(2,1)S(1)}, u32[]{:S(2)}) copy-start(bf16[512,768]{1,0:T(8,128)(2,1)S(1)} %get-tuple-element.13) | copy-start | bytes 2359300
  68.3 10.6 %collective-permute-start.13 = (bf16[512,768]{1,0:T(8,128)(2,1)}, bf16[512,768]{1,0:T(8,128)(2,1)}, u32[]{:S(2)}, u32[]{:S(2)}) collective-permute-start(bf16[512,768]{1,0:T(8,128)(2,1)} %get-tuple-element.23), channel_id=1, source_target_pairs={{0,4},{4,0},{8,12},{12,8},{16,20},{20,16},{24,28},{28,24},{32,36},... | collective-permute-start | bytes 2359304 | tf_op jit(solution)/shard_map/ppermute | solution.py:74
  68.7 10.2 %copy-start.2 = (bf16[512,768]{1,0:T(8,128)(2,1)S(1)}, bf16[512,768]{1,0:T(8,128)(2,1)}, u32[]{:S(2)}) copy-start(bf16[512,768]{1,0:T(8,128)(2,1)} %copy-done.1) | copy-start | bytes 2359300
  68.7 10.2 %copy-start.4 = (bf16[512,768]{1,0:T(8,128)(2,1)S(1)}, bf16[512,768]{1,0:T(8,128)(2,1)}, u32[]{:S(2)}) copy-start(bf16[512,768]{1,0:T(8,128)(2,1)} %copy-done.3) | copy-start | bytes 2359300
  69.5 7.5 %collective-permute-start.8 = (bf16[256,384]{1,0:T(8,128)(2,1)}, bf16[256,384]{1,0:T(8,128)(2,1)S(1)}, u32[]{:S(2)}, u32[]{:S(2)}) collective-permute-start(bf16[256,384]{1,0:T(8,128)(2,1)} %get-tuple-element.26), channel_id=1, source_target_pairs={{0,1},{1,2},{2,3},{3,0},{4,5},{5,6},{6,7},{7,4},{8,9},{9,10},{10,1... | collective-permute-start | bytes 589832 | tf_op jit(solution)/shard_map/ppermute | solution.py:24
  72.3 27.0 %collective-permute-start.12 = (bf16[512,768]{1,0:T(8,128)(2,1)}, bf16[512,768]{1,0:T(8,128)(2,1)S(1)}, u32[]{:S(2)}, u32[]{:S(2)}) collective-permute-start(bf16[512,768]{1,0:T(8,128)(2,1)} %get-tuple-element.22), channel_id=1, source_target_pairs={{0,4},{4,0},{8,12},{12,8},{16,20},{20,16},{24,28},{28,24},{32,36},... | collective-permute-start | bytes 2359304 | tf_op jit(solution)/shard_map/ppermute | solution.py:74
  72.7 14.0 %collective-permute-start.10 = (bf16[256,384]{1,0:T(8,128)(2,1)S(1)}, bf16[256,384]{1,0:T(8,128)(2,1)S(1)}, u32[]{:S(2)}, u32[]{:S(2)}) collective-permute-start(bf16[256,384]{1,0:T(8,128)(2,1)S(1)} %get-tuple-element.27), channel_id=1, source_target_pairs={{0,3},{1,0},{2,1},{3,2},{4,7},{5,4},{6,5},{7,6},{8,11},{9,8},{10,9... | collective-permute-start | bytes 589832 | tf_op jit(solution)/shard_map/ppermute | solution.py:24
  77.4 10.7 %collective-permute-start.9 = (bf16[512,384]{1,0:T(8,128)(2,1)S(1)}, bf16[512,384]{1,0:T(8,128)(2,1)S(1)}, u32[]{:S(2)}, u32[]{:S(2)}) collective-permute-start(bf16[512,384]{1,0:T(8,128)(2,1)S(1)} %fusion.9), channel_id=1, source_target_pairs={{0,1},{1,2},{2,3},{3,0},{4,5},{5,6},{6,7},{7,4},{8,9},{9,10},{10,1... | collective-permute-start | bytes 1179656 | tf_op jit(solution)/shard_map/ppermute | solution.py:24
  80.7 20.7 %collective-permute-start.14 = (bf16[512,768]{1,0:T(8,128)(2,1)S(1)}, bf16[512,768]{1,0:T(8,128)(2,1)S(1)}, u32[]{:S(2)}, u32[]{:S(2)}) collective-permute-start(bf16[512,768]{1,0:T(8,128)(2,1)S(1)} %get-tuple-element.20), channel_id=1, source_target_pairs={{0,8},{4,12},{8,16},{12,20},{16,24},{20,28},{24,32},{28,36},{32,40... | collective-permute-start | bytes 2359304 | tf_op jit(solution)/shard_map/ppermute | solution.py:19
  82.7 24.0 %collective-permute-start.15 = (bf16[512,768]{1,0:T(8,128)(2,1)S(1)}, bf16[512,768]{1,0:T(8,128)(2,1)S(1)}, u32[]{:S(2)}, u32[]{:S(2)}) collective-permute-start(bf16[512,768]{1,0:T(8,128)(2,1)S(1)} %get-tuple-element.21), channel_id=1, source_target_pairs={{8,0},{12,4},{16,8},{20,12},{24,16},{28,20},{32,24},{36,28},{40,32... | collective-permute-start | bytes 2359304 | tf_op jit(solution)/shard_map/ppermute | solution.py:19
  87.0 19.7 %copy-start.7 = (f32[512,768]{1,0:T(8,128)S(1)}, f32[512,768]{1,0:T(8,128)}, u32[]{:S(2)}) copy-start(f32[512,768]{1,0:T(8,128)} %get-tuple-element.11) | copy-start | bytes 4718596
  87.0 11.1 %collective-permute-start.11 = (bf16[512,384]{1,0:T(8,128)(2,1)S(1)}, bf16[512,384]{1,0:T(8,128)(2,1)S(1)}, u32[]{:S(2)}, u32[]{:S(2)}) collective-permute-start(bf16[512,384]{1,0:T(8,128)(2,1)S(1)} %fusion.10), channel_id=1, source_target_pairs={{0,3},{1,0},{2,1},{3,2},{4,7},{5,4},{6,5},{7,6},{8,11},{9,8},{10,9... | collective-permute-start | bytes 1179656 | tf_op jit(solution)/shard_map/ppermute | solution.py:24

commit v3 on v2

--- a/solution.py
+++ b/solution.py
@@ -1,5 +1,3 @@
-import functools
-
 import jax
 import jax.numpy as jnp
 from jax import lax
@@ -35,8 +33,8 @@
     half = rows // 2
     from_prev = ring_shift(cotangent, "head", 1)
     from_next = ring_shift(cotangent, "head", -1)
-    far_a = ring_shift(from_prev[:half], "head", 1)
-    far_b = ring_shift(from_next[half:], "head", -1)
+    far_a = ring_shift(cotangent[:half], "head", 2)
+    far_b = ring_shift(cotangent[half:], "head", -2)
     far = jnp.concatenate([far_a, far_b], axis=0)
     nt = (((1,), (1,)), ((), ()))
     acc = None
@@ -55,17 +53,19 @@
 
     def part(group):
         w_cols = head_slice(out_weight, group % groups, width)
-        return jnp.dot(attn, w_cols, preferred_element_type=jnp.float32)
-
-    far = part(me + 2).astype(jnp.bfloat16)
-    got_a = ring_shift(far[:half], "head", 1)
-    got_b = ring_shift(far[half:], "head", -1)
-    zeros = jnp.zeros((half, width), jnp.float32)
-    up = part(me + 1) + jnp.concatenate([got_a.astype(jnp.float32), zeros], axis=0)
-    down = part(me - 1) + jnp.concatenate([zeros, got_b.astype(jnp.float32)], axis=0)
-    from_prev = ring_shift(up.astype(jnp.bfloat16), "head", 1)
-    from_next = ring_shift(down.astype(jnp.bfloat16), "head", -1)
-    total = part(me) + from_prev.astype(jnp.float32) + from_next.astype(jnp.float32)
+        return jnp.dot(attn, w_cols, preferred_element_type=jnp.float32).astype(jnp.bfloat16)
+
+    far = part(me + 2)
+    got_a = ring_shift(far[:half], "head", 2)
+    got_b = ring_shift(far[half:], "head", -2)
+    from_prev = ring_shift(part(me + 1), "head", 1)
+    from_next = ring_shift(part(me - 1), "head", -1)
+    total = (
+        jnp.dot(attn, head_slice(out_weight, me, width), preferred_element_type=jnp.float32)
+        + from_prev.astype(jnp.float32)
+        + from_next.astype(jnp.float32)
+        + jnp.concatenate([got_a, got_b], axis=0).astype(jnp.float32)
+    )
     return total.astype(jnp.bfloat16)
 
 
@@ -74,37 +74,24 @@
     return lax.ppermute(block, axis, [(i, i ^ 1) for i in range(size)])
 
 
-def pack_heads(keys, values):
-    rows, columns = keys.shape
-    heads = columns // HEAD_DIM
-    k4 = keys.reshape(rows, heads, 1, HEAD_DIM)
-    v4 = values.reshape(rows, heads, 1, HEAD_DIM)
-    return jnp.concatenate([k4, v4], axis=2).reshape(rows, 2 * columns)
-
-
-def unpack_heads(packed):
-    rows, wide = packed.shape
-    heads = wide // (2 * HEAD_DIM)
-    p4 = packed.reshape(rows, heads, 2, HEAD_DIM)
-    return (p4[:, :, 0, :].reshape(rows, heads * HEAD_DIM), p4[:, :, 1, :].reshape(rows, heads * HEAD_DIM))
-
-
-def attn_kernel(sel_ref, q_ref, kv0_ref, c0_ref, c1_ref, c2_ref, c3_ref, g_ref, srow_ref, scol_ref,
-                attn_ref, dq_ref, dkv0_ref, dkv1_ref, dkv2_ref):
+def attn_kernel(sel_ref, q_ref, k0_ref, v0_ref, *refs):
+    cand_k = refs[0:8:2]
+    cand_v = refs[1:8:2]
+    g_ref, srow_ref, scol_ref, attn_ref, dq_ref, dkv0_ref, dkv1_ref, dkv2_ref = refs[8:]
     scale = HEAD_DIM ** (-0.5)
     d = HEAD_DIM
-    cands = (c0_ref, c1_ref, c2_ref, c3_ref)
-
-    def pick(slot):
+    h = pl.program_id(0)
+    heads = pl.num_programs(0)
+
+    def pick(cands, slot):
         idx = sel_ref[slot]
         out = cands[0][...]
         for c in range(1, 4):
             out = jnp.where(idx == c, cands[c][...], out)
         return out
 
-    kv = [kv0_ref[...], pick(0), pick(1)]
-    ks = [x[:, :d] for x in kv]
-    vs = [x[:, d:] for x in kv]
+    ks = [k0_ref[...], pick(cand_k, 0), pick(cand_k, 1)]
+    vs = [v0_ref[...], pick(cand_v, 0), pick(cand_v, 1)]
     q = q_ref[...]
     g = g_ref[...]
     nt = (((1,), (1,)), ((), ()))
@@ -132,6 +119,8 @@
     delta = jnp.sum(attn.astype(jnp.float32) * gf, axis=1, keepdims=True)
     dq = None
     outs = (dkv0_ref, dkv1_ref, dkv2_ref)
+    k_cols = pl.ds(pl.multiple_of(h * d, d), d)
+    v_cols = pl.ds(pl.multiple_of((heads + h) * d, d), d)
     for j in range(3):
         dp = lax.dot_general(g, vs[j], nt, preferred_element_type=jnp.float32)
         ds = (probs[j] * (dp - delta) * scale).astype(jnp.bfloat16)
@@ -139,25 +128,30 @@
         dq = part if dq is None else dq + part
         dk = lax.dot_general(ds, q, tn, preferred_element_type=jnp.float32)
         dv = lax.dot_general(low[j], g, tn, preferred_element_type=jnp.float32)
-        outs[j][:, :d] = dk.astype(outs[j].dtype)
-        outs[j][:, d:] = dv.astype(outs[j].dtype)
+        outs[j][:, k_cols] = dk.astype(outs[j].dtype)
+        outs[j][:, v_cols] = dv.astype(outs[j].dtype)
     dq_ref[...] = dq.astype(jnp.bfloat16)
 
 
-def attention(sel, queries, kv_self, cands, grad_attn, shot_ids):
+def attention(sel, queries, keys, values, cands, grad_attn, shot_ids):
     rows, columns = queries.shape
     heads = columns // HEAD_DIM
     d = HEAD_DIM
-    col = lambda h, s: (0, h)
-    spec_q = pl.BlockSpec((rows, d), col)
-    spec_kv = pl.BlockSpec((rows, 2 * d), col)
+    spec_q = pl.BlockSpec((rows, d), lambda h, s: (0, h))
+    spec_v = pl.BlockSpec((rows, d), lambda h, s: (0, heads + h))
+    spec_wide = pl.BlockSpec((rows, 2 * columns), lambda h, s: (0, 0))
+    cand_specs = []
+    cand_args = []
+    for c in cands:
+        cand_specs += [spec_q, spec_v]
+        cand_args += [c, c]
     grid_spec = pltpu.PrefetchScalarGridSpec(
         num_scalar_prefetch=1,
         grid=(heads,),
-        in_specs=[spec_q, spec_kv, spec_kv, spec_kv, spec_kv, spec_kv, spec_q,
+        in_specs=[spec_q, spec_q, spec_q] + cand_specs + [spec_q,
                   pl.BlockSpec((rows, 1), lambda h, s: (0, 0)),
                   pl.BlockSpec((1, rows), lambda h, s: (0, 0))],
-        out_specs=[spec_q, spec_q, spec_kv, spec_kv, spec_kv],
+        out_specs=[spec_q, spec_q, spec_wide, spec_wide, spec_wide],
     )
     out_shape = [
         jax.ShapeDtypeStruct((rows, columns), jnp.bfloat16),
@@ -175,7 +169,7 @@
         out_shape=out_shape,
         compiler_params=pltpu.CompilerParams(vmem_limit_bytes=48 * 1024 * 1024),
         **kwargs,
-    )(sel, queries, kv_self, *cands, grad_attn, shot_ids.reshape(rows, 1), shot_ids.reshape(1, rows))
+    )(sel, queries, keys, values, *cand_args, grad_attn, shot_ids.reshape(rows, 1), shot_ids.reshape(1, rows))
 
 
 def on_device(queries, keys, values, out_weight, cotangent, routes, shot_ids):
@@ -183,7 +177,7 @@
     tok_rows, columns = queries.shape
     parity = seq_index % 2
     grad_attn = fold_cotangent(cotangent, out_weight)
-    own_kv = pack_heads(keys, values)
+    own_kv = jnp.concatenate([keys, values], axis=1)
     from_left2 = shifted(own_kv, "seq", 2)
     from_right2 = shifted(own_kv, "seq", -2)
     partner_own = partner_swap(own_kv, "seq")
@@ -194,7 +188,7 @@
     sel = jnp.where(offs == -2, 0, jnp.where(offs == 2, 3, jnp.where(offs == partner_off, 1, 2)))
     sel = sel.astype(jnp.int32)
     cands = (from_left2, partner_own, partner_relay, from_right2)
-    attn, grad_q, self_term, term1, term2 = attention(sel, queries, own_kv, cands, grad_attn, shot_ids)
+    attn, grad_q, self_term, term1, term2 = attention(sel, queries, keys, values, cands, grad_attn, shot_ids)
     attn_out = project_out(attn, out_weight)
     zero = jnp.zeros_like(term1)
 
@@ -217,7 +211,8 @@
         + got_from_left.astype(jnp.float32)
         + got_from_right.astype(jnp.float32)
     )
-    grad_keys, grad_values = unpack_heads(total.astype(jnp.bfloat16))
+    rounded = total.astype(jnp.bfloat16)
+    grad_keys, grad_values = rounded[:, :columns], rounded[:, columns:]
     return (attn_out, grad_q, grad_keys, grad_values)
 
 

time: 113 us -> 111 us (0.982)
  local copies, waits for them, and re-layouts: 11.7 us -> 6.44 us
  waiting for transfers between devices: 43.2 us -> 40 us
  starting transfers between devices: 21.5 us -> 24.1 us
  other arithmetic: 5.96 us -> 8.37 us
    unnamed x24 -> x27, local copies, waits for them, and re-layouts: 6.55 us -> 2.12 us
    ppermute x4, waiting for transfers between devices: 25.1 us -> 21.4 us  [shifted(): return lax.ppermute(block, axis, route)]
    ppermute x8, starting transfers between devices: 8.49 us -> 10.8 us  [ring_shift(): lax.ppermute(block, axis, [(i, (i + distance) % size) for i in range(size)])]
    dot_general x4, matrix products: 2.36 us -> 4.36 us  [the longest x1 2.44 us: project_out(): jnp.dot(attn, head_slice(out_weight, me, width), preferred_element_type=j...]
    convert_element_type x1, other arithmetic: 0.39 us -> 1.58 us  [on_device(): rounded = total.astype(jnp.bfloat16)]
    convert_element_type x1, other arithmetic: 1.78 us -> 2.95 us  [on_device(): got_from_left = shifted(up_plus.astype(jnp.bfloat16), 'seq', 2)]
    dot_general x4, matrix products: 5.76 us -> 4.6 us  [fold_cotangent(): lax.dot_general(piece, w_cols, nt, preferred_element_type=jnp.float32)]
    slice x4 -> x3, local copies, waits for them, and re-layouts: 2.78 us -> 1.78 us  [the longest x1 0.96 us: on_device(): grad_keys, grad_values = (rounded[:, :columns], rounded[:, columns:])]
  transfers between devices with their start and end apart: 16 -> 16, of which waited for: 9 -> 6; matrix products, arithmetic and copies ran while one was open for 13% -> 14% of each run, Pallas kernels for 0% -> 0%
where the time goes in v3:
time: 111 us
  waiting for transfers between devices  40 us (36%)
  starting transfers between devices  24.1 us (22%)
  Pallas kernels  16.3 us (15%)
  matrix products  8.96 us (8%)
  other arithmetic  8.37 us (8%)
  local copies, waits for them, and re-layouts  6.44 us (6%)
  between operations  6.32 us (6%)
    ppermute x4, waiting for transfers between devices, shifted(): return lax.ppermute(block, axis, route)  21.4 us
    ppermute x8, waiting for transfers between devices, ring_shift(): lax.ppermute(block, axis, [(i, (i + distance) % size) for i in range(size)])  18.6 us
    pallas_call x1, Pallas kernels, attention(): pl.pallas_call(attn_kernel, grid_spec=grid_spec, out_shape=out_shape, com...  16.3 us
    ppermute x4, starting transfers between devices, shifted(): return lax.ppermute(block, axis, route)  12.7 us
    ppermute x8, starting transfers between devices, ring_shift(): lax.ppermute(block, axis, [(i, (i + distance) % size) for i in range(size)])  10.8 us
    dot_general x4, matrix products, fold_cotangent(): lax.dot_general(piece, w_cols, nt, preferred_element_type=jnp.float32)  4.6 us
    convert_element_type x1, other arithmetic, on_device(): got_from_left = shifted(up_plus.astype(jnp.bfloat16), 'seq', 2)  2.95 us
    dot_general x1, matrix products, project_out(): jnp.dot(attn, head_slice(out_weight, me, width), preferred_element_type=j...  2.44 us
  transfers between devices with their start and end apart: 16, of which 6 were waited for; matrix products, arithmetic and copies ran while one was open for 14% of the time, Pallas kernels for 0%

profile of v3, /device:TPU:126, one launch (start us, length us, event | category | flops | bytes accessed | tf_op | source)
XLA Modules:
  0.0 110.6 jit_solution(14545850139738626482)
XLA Ops:
  0.7 2.0 %constant_dynamic-update-slice_fusion.1 = bf16[512,768]{1,0:T(8,128)(2,1)} fusion(bf16[512,384]{1,0:T(8,128)(2,1)} %k0_ref.1), kind=kLoop, calls=%fused_computation.38 | loop fusion | bytes 786432
  2.6 1.8 %constant_dynamic-update-slice_fusion = bf16[512,768]{1,0:T(8,128)(2,1)} fusion(bf16[512,768]{1,0:T(8,128)(2,1)} %constant_dynamic-update-slice_fusion.1, bf16[512,384]{1,0:T(8,128)(2,1)} %v0_ref.1), kind=kLoop, calls=%fused_computation.37 | loop fusion | bytes 786432 | tf_op jit(solution)/shard_map/concatenate | solution.py:180
  4.4 4.9 %collective-permute-start = (bf16[512,768]{1,0:T(8,128)(2,1)}, bf16[512,768]{1,0:T(8,128)(2,1)S(1)}, u32[]{:S(2)}, u32[]{:S(2)}) collective-permute-start(bf16[512,768]{1,0:T(8,128)(2,1)} %constant_dynamic-update-slice_fusion), channel_id=1, source_target_pairs={{0,8},{4,12},{8,16},{12,20},{16,24},{20,28},{24,32},{28,36},{32,40... | collective-permute-start | bytes 2359304 | tf_op jit(solution)/shard_map/ppermute | solution.py:17
  9.4 1.9 %collective-permute-start.2 = (bf16[512,768]{1,0:T(8,128)(2,1)}, bf16[512,768]{1,0:T(8,128)(2,1)}, u32[]{:S(2)}, u32[]{:S(2)}) collective-permute-start(bf16[512,768]{1,0:T(8,128)(2,1)} %constant_dynamic-update-slice_fusion), channel_id=1, source_target_pairs={{8,0},{12,4},{16,8},{20,12},{24,16},{28,20},{32,24},{36,28},{40,32... | collective-permute-start | bytes 2359304 | tf_op jit(solution)/shard_map/ppermute | solution.py:17
  11.7 0.8 fusion.37
  12.5 2.6 %collective-permute-start.6 = (bf16[256,384]{1,0:T(8,128)(2,1)}, bf16[256,384]{1,0:T(8,128)(2,1)}, u32[]{:S(2)}, u32[]{:S(2)}) collective-permute-start(bf16[256,384]{1,0:T(8,128)(2,1)} %get-tuple-element.24), channel_id=1, source_target_pairs={{0,2},{1,3},{2,0},{3,1},{4,6},{5,7},{6,4},{7,5},{8,10},{9,11},{10,... | collective-permute-start | bytes 589832 | tf_op jit(solution)/shard_map/ppermute | solution.py:22
  15.3 1.3 %fusion.15 = f32[384,512]{0,1:T(8,128)} fusion(bf16[512,384]{1,0:T(8,128)(2,1)S(1)} %copy-done.10, bf16[384,1536]{1,0:T(8,128)(2,1)S(1)} %copy-done, s32[]{:T(128)S(6)} %select_n.150), kind=kOutput, calls=%fused_computation.29 | convolution fusion | flops 150994944 | bytes 1474564 | tf_op jit(solution)/shard_map/dot_general | solution.py:43
  16.6 9.8 %collective-permute-done.refs_0_.refs_1_ = bf16[512,768]{1,0:T(8,128)(2,1)S(1)} collective-permute-done((bf16[512,768]{1,0:T(8,128)(2,1)}, bf16[512,768]{1,0:T(8,128)(2,1)S(1)}, u32[]{:S(2)}, u32[]{:S(2)}) %collective-permute-start) | collective-permute-done | bytes 786464 | tf_op jit(solution)/shard_map/ppermute | solution.py:17
  26.5 1.2 %collective-permute-start.7 = (bf16[256,384]{1,0:T(8,128)(2,1)}, bf16[256,384]{1,0:T(8,128)(2,1)}, u32[]{:S(2)}, u32[]{:S(2)}) collective-permute-start(bf16[256,384]{1,0:T(8,128)(2,1)} %get-tuple-element.25), channel_id=1, source_target_pairs={{0,2},{1,3},{2,0},{3,1},{4,6},{5,7},{6,4},{7,5},{8,10},{9,11},{10,... | collective-permute-start | bytes 589832 | tf_op jit(solution)/shard_map/ppermute | solution.py:22
  27.7 6.2 %collective-permute-done.2.refs_6_.refs_7_ = bf16[512,768]{1,0:T(8,128)(2,1)} collective-permute-done((bf16[512,768]{1,0:T(8,128)(2,1)}, bf16[512,768]{1,0:T(8,128)(2,1)}, u32[]{:S(2)}, u32[]{:S(2)}) %collective-permute-start.2) | collective-permute-done | bytes 786464 | tf_op jit(solution)/shard_map/ppermute | solution.py:17
  33.9 2.1 %broadcast_select_fusion.2 = bf16[512,768]{1,0:T(8,128)(2,1)} fusion(bf16[512,768]{1,0:T(8,128)(2,1)} %collective-permute-done.2.refs_6_.refs_7_, bf16[512,768]{1,0:T(8,128)(2,1)S(1)} %collective-permute-done.refs_0_.refs_1_, pred[]{:T(512)S(6)} %eq.96), kind=kLoop, calls=%fused_computation.23 | loop fusion | flops 393216 | bytes 2359297 | tf_op jit(solution)/shard_map/jit(_where)/select_n | solution.py:184
  36.0 0.6 fusion.38
  39.5 0.8 collective-permute-start.5
  40.3 1.4 %fusion.10 = f32[512,384]{1,0:T(8,128)S(1)} fusion(bf16[256,384]{1,0:T(8,128)(2,1)} %collective-permute-done.7, bf16[256,384]{1,0:T(8,128)(2,1)} %collective-permute-done.6, bf16[384,1536]{1,0:T(8,128)(2,1)S(1)} %copy-done, s32[]{:T(128)S(6)} %select_n.156), kind=kOutput, calls=%fused_computation.24 | convolution fusion | flops 151781376 | bytes 1474564 | tf_op jit(solution)/shard_map/dot_general | solution.py:43
  41.8 1.4 %convolution_add_fusion.2 = f32[384,512]{0,1:T(8,128)S(1)} fusion(f32[384,512]{0,1:T(8,128)S(1)} %copy-done.9, bf16[512,384]{1,0:T(8,128)(2,1)} %collective-permute-done.4, bf16[384,1536]{1,0:T(8,128)(2,1)S(1)} %copy-done, s32[]{:T(128)S(6)} %select_n.152), kind=kOutput, calls=%fused_computation.10 | convolution fusion | flops 151191552 | bytes 2260996 | tf_op jit(solution)/shard_map/dot_general | solution.py:43
  43.2 9.1 %collective-permute-done.5 = bf16[512,384]{1,0:T(8,128)(2,1)S(1)} collective-permute-done((bf16[512,384]{1,0:T(8,128)(2,1)S(1)}, bf16[512,384]{1,0:T(8,128)(2,1)S(1)}, u32[]{:S(2)}, u32[]{:S(2)}) %collective-permute-start.5) | collective-permute-done | bytes 393248 | tf_op jit(solution)/shard_map/ppermute | solution.py:22
  52.3 0.4 fusion.9.refs_8_
  52.8 16.3 %shard_map.102 = (bf16[512,384]{1,0:T(8,128)(2,1)S(1)}, bf16[512,384]{1,0:T(8,128)(2,1)}, f32[512,768]{1,0:T(8,128)}, bf16[512,768]{1,0:T(8,128)(2,1)S(1)}, bf16[512,768]{1,0:T(8,128)(2,1)S(1)}) custom-call(s32[2]{0:T(128)S(1)} %get-tuple-element.14.sel_ref, bf16[512,384]{1,0:T(8,128)(2,1)S(1)} %copy-done.7, bf16[512,384]{1,0:T(8,128)(2,1)S(1)} %copy-done.5, ...), custom_call_target="tpu_custom_call" | custom-call | tf_op jit(solution)/shard_map/pallas_call | solution.py:166
  69.1 1.5 %broadcast_select_fusion.1 = (bf16[512,768]{1,0:T(8,128)(2,1)}, bf16[512,768]{1,0:T(8,128)(2,1)}) fusion(pred[]{:T(512)S(6)} %eq.96, bf16[512,768]{1,0:T(8,128)(2,1)S(1)} %get-tuple-element.12, bf16[512,768]{1,0:T(8,128)(2,1)S(1)} %get-tuple-element.13, pred[]{:T(512)} %bitcast.4, pred[]{:T(512)} %bitcast.3, pred[]{:T(512)} %bitcast.6, pred[]{:T(512)} %bitcast.5), kind=kLoop, calls=%fused_computation.22 | loop fusion | flops 2359296 | bytes 3145733 | tf_op jit(solution)/shard_map/jit(_where)/select_n | solution.py:200
  73.5 0.6 collective-permute-start.12
  74.8 3.5 %collective-permute-start.11 = (bf16[256,384]{1,0:T(8,128)(2,1)S(1)}, bf16[256,384]{1,0:T(8,128)(2,1)}, u32[]{:S(2)}, u32[]{:S(2)}) collective-permute-start(bf16[256,384]{1,0:T(8,128)(2,1)S(1)} %get-tuple-element.23), channel_id=1, source_target_pairs={{0,2},{1,3},{2,0},{3,1},{4,6},{5,7},{6,4},{7,5},{8,10},{9,11},{10,... | collective-permute-start | bytes 589832 | tf_op jit(solution)/shard_map/ppermute | solution.py:22
  78.7 3.0 %fusion.1 = (bf16[512,768]{1,0:T(8,128)(2,1)}, bf16[512,768]{1,0:T(8,128)(2,1)}) fusion(bf16[512,768]{1,0:T(8,128)(2,1)} %collective-permute-done.13, bf16[512,768]{1,0:T(8,128)(2,1)S(1)} %copy-done.2, bf16[512,768]{1,0:T(8,128)(2,1)S(1)} %copy-done.4, pred[]{:T(512)} %bitcast.8, pred[]{:T(512)} %bitcast.7, pred[]{:T(512)S(6)} %eq.96, pred[]{:T(512)S(6)} %eq.113, ...), kind=kLoop, calls=%fused_computation.3 | loop fusion | flops 5111808 | bytes 3932166 | tf_op jit(solution)/shard_map/convert_element_type | solution.py:206
  81.7 1.9 %collective-permute-start.14 = (bf16[512,768]{1,0:T(8,128)(2,1)}, bf16[512,768]{1,0:T(8,128)(2,1)S(1)}, u32[]{:S(2)}, u32[]{:S(2)}) collective-permute-start(bf16[512,768]{1,0:T(8,128)(2,1)} %get-tuple-element.16), channel_id=1, source_target_pairs={{0,8},{4,12},{8,16},{12,20},{16,24},{20,28},{24,32},{28,36},{32,40... | collective-permute-start | bytes 2359304 | tf_op jit(solution)/shard_map/ppermute | solution.py:17
  83.6 3.9 %collective-permute-start.15 = (bf16[512,768]{1,0:T(8,128)(2,1)}, bf16[512,768]{1,0:T(8,128)(2,1)}, u32[]{:S(2)}, u32[]{:S(2)}) collective-permute-start(bf16[512,768]{1,0:T(8,128)(2,1)} %get-tuple-element.17), channel_id=1, source_target_pairs={{8,0},{12,4},{16,8},{20,12},{24,16},{28,20},{32,24},{36,28},{40,32... | collective-permute-start | bytes 2359304 | tf_op jit(solution)/shard_map/ppermute | solution.py:17
  87.5 1.1 %convolution_convert_fusion.1 = bf16[512,384]{1,0:T(8,128)(2,1)} fusion(bf16[512,384]{1,0:T(8,128)(2,1)S(1)} %get-tuple-element.9, bf16[384,1536]{1,0:T(8,128)(2,1)S(1)} %copy-done, s32[]{:T(128)S(6)} %select_n.152), kind=kOutput, calls=%fused_computation.17 | convolution fusion | flops 151191552 | bytes 1081348 | tf_op jit(solution)/shard_map/dot_general | solution.py:56
  88.7 2.0 %collective-permute-start.9 = (bf16[512,384]{1,0:T(8,128)(2,1)}, bf16[512,384]{1,0:T(8,128)(2,1)}, u32[]{:S(2)}, u32[]{:S(2)}) collective-permute-start(bf16[512,384]{1,0:T(8,128)(2,1)} %convolution_convert_fusion.1), channel_id=1, source_target_pairs={{0,3},{1,0},{2,1},{3,2},{4,7},{5,4},{6,5},{7,6},{8,11},{9,8},{10,9... | collective-permute-start | bytes 1179656 | tf_op jit(solution)/shard_map/ppermute | solution.py:22
  90.7 8.0 %collective-permute-done.8 = bf16[512,384]{1,0:T(8,128)(2,1)} collective-permute-done((bf16[512,384]{1,0:T(8,128)(2,1)S(1)}, bf16[512,384]{1,0:T(8,128)(2,1)}, u32[]{:S(2)}, u32[]{:S(2)}) %collective-permute-start.8) | collective-permute-done | bytes 393248 | tf_op jit(solution)/shard_map/ppermute | solution.py:22
  98.7 1.5 %collective-permute-done.9 = bf16[512,384]{1,0:T(8,128)(2,1)} collective-permute-done((bf16[512,384]{1,0:T(8,128)(2,1)}, bf16[512,384]{1,0:T(8,128)(2,1)}, u32[]{:S(2)}, u32[]{:S(2)}) %collective-permute-start.9) | collective-permute-done | bytes 393248 | tf_op jit(solution)/shard_map/ppermute | solution.py:22
  100.2 2.4 %fusion.8 = bf16[512,384]{1,0:T(8,128)(2,1)} fusion(bf16[512,384]{1,0:T(8,128)(2,1)S(1)} %get-tuple-element.9, bf16[512,384]{1,0:T(8,128)(2,1)} %collective-permute-done.9, bf16[512,384]{1,0:T(8,128)(2,1)} %collective-permute-done.8, bf16[256,384]{1,0:T(8,128)(2,1)} %collective-permute-done.11, bf16[256,384]{1,0:T(8,128)(2,1)} %collective-permute-done.10, ...), kind=kOutput, calls=%fused_computation.14 | convolution fusion | flops 152961024 | bytes 2260996 | tf_op jit(solution)/shard_map/dot_general | solution.py:64
  102.7 5.4 %collective-permute-done.15 = bf16[512,768]{1,0:T(8,128)(2,1)} collective-permute-done((bf16[512,768]{1,0:T(8,128)(2,1)}, bf16[512,768]{1,0:T(8,128)(2,1)}, u32[]{:S(2)}, u32[]{:S(2)}) %collective-permute-start.15) | collective-permute-done | bytes 786464 | tf_op jit(solution)/shard_map/ppermute | solution.py:17
  108.0 1.6 %add_convert_fusion = bf16[512,768]{1,0:T(8,128)(2,1)S(1)} fusion(bf16[512,768]{1,0:T(8,128)(2,1)} %collective-permute-done.15, bf16[512,768]{1,0:T(8,128)(2,1)S(1)} %collective-permute-done.14, f32[512,768]{1,0:T(8,128)S(1)} %copy-done.11, bf16[512,768]{1,0:T(8,128)(2,1)S(1)} %collective-permute-done.12), kind=kLoop, calls=%fused_computation.6 | loop fusion | flops 2752512 | bytes 4718592 | tf_op jit(solution)/shard_map/convert_element_type | solution.py:214
  109.6 1.0 fusion.35
  (47 shorter events, 2.1 us)
Async XLA Ops:
  0.6 14.6 %copy-start = (bf16[384,1536]{1,0:T(8,128)(2,1)S(1)}, bf16[384,1536]{1,0:T(8,128)(2,1)}, u32[]{:S(2)}) copy-start(bf16[384,1536]{1,0:T(8,128)(2,1)} %param.10) | copy-start | bytes 3538948
  0.6 10.8 %copy-start.10 = (bf16[512,384]{1,0:T(8,128)(2,1)S(1)}, bf16[512,384]{1,0:T(8,128)(2,1)}, u32[]{:S(2)}) copy-start(bf16[512,384]{1,0:T(8,128)(2,1)} %param.11) | copy-start | bytes 1179652
  0.7 14.4 %copy-start.12 = (s32[64,2]{0,1:T(2,128)S(1)}, s32[64,2]{0,1:T(2,128)}, u32[]{:S(2)}) copy-start(s32[64,2]{0,1:T(2,128)} %param.12) | copy-start | bytes 1540
  4.4 22.0 %collective-permute-start = (bf16[512,768]{1,0:T(8,128)(2,1)}, bf16[512,768]{1,0:T(8,128)(2,1)S(1)}, u32[]{:S(2)}, u32[]{:S(2)}) collective-permute-start(bf16[512,768]{1,0:T(8,128)(2,1)} %constant_dynamic-update-slice_fusion), channel_id=1, source_target_pairs={{0,8},{4,12},{8,16},{12,20},{16,24},{20,28},{24,32},{28,36},{32,40... | collective-permute-start | bytes 2359304 | tf_op jit(solution)/shard_map/ppermute | solution.py:17
  9.4 24.5 %collective-permute-start.2 = (bf16[512,768]{1,0:T(8,128)(2,1)}, bf16[512,768]{1,0:T(8,128)(2,1)}, u32[]{:S(2)}, u32[]{:S(2)}) collective-permute-start(bf16[512,768]{1,0:T(8,128)(2,1)} %constant_dynamic-update-slice_fusion), channel_id=1, source_target_pairs={{8,0},{12,4},{16,8},{20,12},{24,16},{28,20},{32,24},{36,28},{40,32... | collective-permute-start | bytes 2359304 | tf_op jit(solution)/shard_map/ppermute | solution.py:17
  11.3 41.5 %collective-permute-start.1 = (bf16[512,768]{1,0:T(8,128)(2,1)}, bf16[512,768]{1,0:T(8,128)(2,1)S(1)}, u32[]{:S(2)}, u32[]{:S(2)}) collective-permute-start(bf16[512,768]{1,0:T(8,128)(2,1)} %constant_dynamic-update-slice_fusion), channel_id=1, source_target_pairs={{0,4},{4,0},{8,12},{12,8},{16,20},{20,16},{24,28},{28,24},{32,36},... | collective-permute-start | bytes 2359304 | tf_op jit(solution)/shard_map/ppermute | solution.py:74
  11.4 30.4 %collective-permute-start.4 = (bf16[512,384]{1,0:T(8,128)(2,1)S(1)}, bf16[512,384]{1,0:T(8,128)(2,1)}, u32[]{:S(2)}, u32[]{:S(2)}) collective-permute-start(bf16[512,384]{1,0:T(8,128)(2,1)S(1)} %copy-done.10), channel_id=1, source_target_pairs={{0,1},{1,2},{2,3},{3,0},{4,5},{5,6},{6,7},{7,4},{8,9},{9,10},{10,1... | collective-permute-start | bytes 1179656 | tf_op jit(solution)/shard_map/ppermute | solution.py:22
  12.5 27.0 %collective-permute-start.6 = (bf16[256,384]{1,0:T(8,128)(2,1)}, bf16[256,384]{1,0:T(8,128)(2,1)}, u32[]{:S(2)}, u32[]{:S(2)}) collective-permute-start(bf16[256,384]{1,0:T(8,128)(2,1)} %get-tuple-element.24), channel_id=1, source_target_pairs={{0,2},{1,3},{2,0},{3,1},{4,6},{5,7},{6,4},{7,5},{8,10},{9,11},{10,... | collective-permute-start | bytes 589832 | tf_op jit(solution)/shard_map/ppermute | solution.py:22
  26.5 12.8 %copy-start.8 = (s32[512]{0:T(512)S(1)}, s32[512]{0:T(512)}, u32[]{:S(2)}) copy-start(s32[512]{0:T(512)} %param.13) | copy-start | bytes 6148
  26.5 13.9 %collective-permute-start.7 = (bf16[256,384]{1,0:T(8,128)(2,1)}, bf16[256,384]{1,0:T(8,128)(2,1)}, u32[]{:S(2)}, u32[]{:S(2)}) collective-permute-start(bf16[256,384]{1,0:T(8,128)(2,1)} %get-tuple-element.25), channel_id=1, source_target_pairs={{0,2},{1,3},{2,0},{3,1},{4,6},{5,7},{6,4},{7,5},{8,10},{9,11},{10,... | collective-permute-start | bytes 589832 | tf_op jit(solution)/shard_map/ppermute | solution.py:22
  36.0 16.7 %collective-permute-start.3 = (bf16[512,768]{1,0:T(8,128)(2,1)}, bf16[512,768]{1,0:T(8,128)(2,1)}, u32[]{:S(2)}, u32[]{:S(2)}) collective-permute-start(bf16[512,768]{1,0:T(8,128)(2,1)} %broadcast_select_fusion.2), channel_id=1, source_target_pairs={{0,4},{4,0},{8,12},{12,8},{16,20},{20,16},{24,28},{28,24},{32,36},... | collective-permute-start | bytes 2359304 | tf_op jit(solution)/shard_map/ppermute | solution.py:74
  39.5 2.3 %copy-start.9 = (f32[384,512]{0,1:T(8,128)S(1)}, f32[384,512]{0,1:T(8,128)}, u32[]{:S(2)}) copy-start(f32[384,512]{0,1:T(8,128)} %fusion.15) | copy-start | bytes 2359300
  39.5 12.8 %collective-permute-start.5 = (bf16[512,384]{1,0:T(8,128)(2,1)S(1)}, bf16[512,384]{1,0:T(8,128)(2,1)S(1)}, u32[]{:S(2)}, u32[]{:S(2)}) collective-permute-start(bf16[512,384]{1,0:T(8,128)(2,1)S(1)} %copy-done.10), channel_id=1, source_target_pairs={{0,3},{1,0},{2,1},{3,2},{4,7},{5,4},{6,5},{7,6},{8,11},{9,8},{10,9... | collective-permute-start | bytes 1179656 | tf_op jit(solution)/shard_map/ppermute | solution.py:22
  43.2 9.6 %copy-start.5 = (bf16[512,384]{1,0:T(8,128)(2,1)S(1)}, bf16[512,384]{1,0:T(8,128)(2,1)}, u32[]{:S(2)}) copy-start(bf16[512,384]{1,0:T(8,128)(2,1)} %k0_ref.1) | copy-start | bytes 1179652
  43.2 9.6 %copy-start.6 = (bf16[512,384]{1,0:T(8,128)(2,1)S(1)}, bf16[512,384]{1,0:T(8,128)(2,1)}, u32[]{:S(2)}) copy-start(bf16[512,384]{1,0:T(8,128)(2,1)} %v0_ref.1) | copy-start | bytes 1179652
  43.2 9.6 %copy-start.7 = (bf16[512,384]{1,0:T(8,128)(2,1)S(1)}, bf16[512,384]{1,0:T(8,128)(2,1)}, u32[]{:S(2)}) copy-start(bf16[512,384]{1,0:T(8,128)(2,1)} %q_ref.1) | copy-start | bytes 1179652
  69.1 1.5 %copy-start.1 = (bf16[512,768]{1,0:T(8,128)(2,1)}, bf16[512,768]{1,0:T(8,128)(2,1)S(1)}, u32[]{:S(2)}) copy-start(bf16[512,768]{1,0:T(8,128)(2,1)S(1)} %get-tuple-element.12) | copy-start | bytes 2359300
  69.1 1.7 %copy-start.3 = (bf16[512,768]{1,0:T(8,128)(2,1)}, bf16[512,768]{1,0:T(8,128)(2,1)S(1)}, u32[]{:S(2)}) copy-start(bf16[512,768]{1,0:T(8,128)(2,1)S(1)} %get-tuple-element.13) | copy-start | bytes 2359300
  70.8 7.9 %collective-permute-start.13 = (bf16[512,768]{1,0:T(8,128)(2,1)}, bf16[512,768]{1,0:T(8,128)(2,1)}, u32[]{:S(2)}, u32[]{:S(2)}) collective-permute-start(bf16[512,768]{1,0:T(8,128)(2,1)} %get-tuple-element.19), channel_id=1, source_target_pairs={{0,4},{4,0},{8,12},{12,8},{16,20},{20,16},{24,28},{28,24},{32,36},... | collective-permute-start | bytes 2359304 | tf_op jit(solution)/shard_map/ppermute | solution.py:74
  73.5 29.2 %collective-permute-start.12 = (bf16[512,768]{1,0:T(8,128)(2,1)}, bf16[512,768]{1,0:T(8,128)(2,1)S(1)}, u32[]{:S(2)}, u32[]{:S(2)}) collective-permute-start(bf16[512,768]{1,0:T(8,128)(2,1)} %get-tuple-element.18), channel_id=1, source_target_pairs={{0,4},{4,0},{8,12},{12,8},{16,20},{20,16},{24,28},{28,24},{32,36},... | collective-permute-start | bytes 2359304 | tf_op jit(solution)/shard_map/ppermute | solution.py:74
  74.4 4.3 %copy-start.2 = (bf16[512,768]{1,0:T(8,128)(2,1)S(1)}, bf16[512,768]{1,0:T(8,128)(2,1)}, u32[]{:S(2)}) copy-start(bf16[512,768]{1,0:T(8,128)(2,1)} %copy-done.1) | copy-start | bytes 2359300
  74.5 4.3 %copy-start.4 = (bf16[512,768]{1,0:T(8,128)(2,1)S(1)}, bf16[512,768]{1,0:T(8,128)(2,1)}, u32[]{:S(2)}) copy-start(bf16[512,768]{1,0:T(8,128)(2,1)} %copy-done.3) | copy-start | bytes 2359300
  74.5 14.2 %collective-permute-start.10 = (bf16[256,384]{1,0:T(8,128)(2,1)S(1)}, bf16[256,384]{1,0:T(8,128)(2,1)}, u32[]{:S(2)}, u32[]{:S(2)}) collective-permute-start(bf16[256,384]{1,0:T(8,128)(2,1)S(1)} %get-tuple-element.22), channel_id=1, source_target_pairs={{0,2},{1,3},{2,0},{3,1},{4,6},{5,7},{6,4},{7,5},{8,10},{9,11},{10,... | collective-permute-start | bytes 589832 | tf_op jit(solution)/shard_map/ppermute | solution.py:22
  74.8 13.9 %collective-permute-start.11 = (bf16[256,384]{1,0:T(8,128)(2,1)S(1)}, bf16[256,384]{1,0:T(8,128)(2,1)}, u32[]{:S(2)}, u32[]{:S(2)}) collective-permute-start(bf16[256,384]{1,0:T(8,128)(2,1)S(1)} %get-tuple-element.23), channel_id=1, source_target_pairs={{0,2},{1,3},{2,0},{3,1},{4,6},{5,7},{6,4},{7,5},{8,10},{9,11},{10,... | collective-permute-start | bytes 589832 | tf_op jit(solution)/shard_map/ppermute | solution.py:22
  81.7 21.0 %collective-permute-start.14 = (bf16[512,768]{1,0:T(8,128)(2,1)}, bf16[512,768]{1,0:T(8,128)(2,1)S(1)}, u32[]{:S(2)}, u32[]{:S(2)}) collective-permute-start(bf16[512,768]{1,0:T(8,128)(2,1)} %get-tuple-element.16), channel_id=1, source_target_pairs={{0,8},{4,12},{8,16},{12,20},{16,24},{20,28},{24,32},{28,36},{32,40... | collective-permute-start | bytes 2359304 | tf_op jit(solution)/shard_map/ppermute | solution.py:17
  83.6 24.4 %collective-permute-start.15 = (bf16[512,768]{1,0:T(8,128)(2,1)}, bf16[512,768]{1,0:T(8,128)(2,1)}, u32[]{:S(2)}, u32[]{:S(2)}) collective-permute-start(bf16[512,768]{1,0:T(8,128)(2,1)} %get-tuple-element.17), channel_id=1, source_target_pairs={{8,0},{12,4},{16,8},{20,12},{24,16},{28,20},{32,24},{36,28},{40,32... | collective-permute-start | bytes 2359304 | tf_op jit(solution)/shard_map/ppermute | solution.py:17
  88.7 10.0 %collective-permute-start.8 = (bf16[512,384]{1,0:T(8,128)(2,1)S(1)}, bf16[512,384]{1,0:T(8,128)(2,1)}, u32[]{:S(2)}, u32[]{:S(2)}) collective-permute-start(bf16[512,384]{1,0:T(8,128)(2,1)S(1)} %convolution_convert_fusion.2), channel_id=1, source_target_pairs={{0,1},{1,2},{2,3},{3,0},{4,5},{5,6},{6,7},{7,4},{8,9},{9,10},{10,1... | collective-permute-start | bytes 1179656 | tf_op jit(solution)/shard_map/ppermute | solution.py:22
  88.7 11.5 %collective-permute-start.9 = (bf16[512,384]{1,0:T(8,128)(2,1)}, bf16[512,384]{1,0:T(8,128)(2,1)}, u32[]{:S(2)}, u32[]{:S(2)}) collective-permute-start(bf16[512,384]{1,0:T(8,128)(2,1)} %convolution_convert_fusion.1), channel_id=1, source_target_pairs={{0,3},{1,0},{2,1},{3,2},{4,7},{5,4},{6,5},{7,6},{8,11},{9,8},{10,9... | collective-permute-start | bytes 1179656 | tf_op jit(solution)/shard_map/ppermute | solution.py:22
  90.7 17.3 %copy-start.11 = (f32[512,768]{1,0:T(8,128)S(1)}, f32[512,768]{1,0:T(8,128)}, u32[]{:S(2)}) copy-start(f32[512,768]{1,0:T(8,128)} %get-tuple-element.11) | copy-start | bytes 4718596
